TPU v7x, 1024 devices: a whole 8x8x8 slice. The times are simulated.
1024 devices in a mesh: box: 32 (over z, x_lo), param: 32 (over y, x_hi, core).
Axes of the slice: x: 8 (x_hi: 2, x_lo: 4; x = x_hi * 4 + x_lo), y: 8, z: 8, core: 2. Of those that a mesh axis runs over, the one named last changes fastest.
Arguments:
- traces: float32 [32, 32, 512, 256], P('box', 'param'), may hold values from -6 to 6
- owners: int32 [32, 32, 512, 1], P('box', 'param'), may hold values from 0 to 31; in each aligned block of 512 rows (0 to 511, 512 to 1023, ..., all dimensions but the last counted through in order) at most 32 rows name the same one
- counts: int32 [32, 32], P('box', 'param'), may hold values from 128 to 512, as said below
- pair_table: int32 [32, 32, 32, 32], P('box', 'param'), may hold values from 0 to 511
- anterp: float32 [256, 512], replicated, may hold values from -0.375 to 0.375
- interp: float32 [2, 512, 256], replicated, may hold values from -0.25 to 0.25
- phase: float32 [32, 32, 3, 512, 256], P('box', 'param'), may hold values from -3.140625 to 3.140625
Outputs:
- weights_out: float32 [32, 32, 2, 512, 256], P('box', 'param')
Inputs may be any that keep to these rules, and one draw needn't show every extreme that they name: `owners`: in the 512 rows of one device no owner is named more than 32 times, a bound that some block reaches. `counts`: some device has all 512 blocks live in every draw.
All inputs are finite; a program needn't handle non-finite values.
Results may differ from a plain program's by a relative error of at most 0.00011.
Values sent between devices are 32-bit elements; how exact they have to be, the bound alone decides.
No kernel may reach another device: no remote copies, remote signals or barrier semaphores. Data moves between devices by JAX's collectives and lax.ppermute only.
A program may use at most 32 MiB of HBM per device.

v0:
```python
import jax
import jax.numpy as jnp
from jax import lax
from jax.sharding import PartitionSpec as P


LEVELS = 3
CHUNK_ROWS = (48, 72, 80, 56)
CHUNKS = len(CHUNK_ROWS)


HIGH = lax.Precision.HIGHEST


def swapped(x, axis, bit):
    return lax.ppermute(x, axis, [(i, i ^ 1 << bit) for i in range(lax.axis_size(axis))])


def rotate(weights_now, cosine, sine_part):
    real_part = weights_now[0]
    imag_part = weights_now[1]
    return jnp.stack(
        [real_part * cosine - imag_part * sine_part, real_part * sine_part + imag_part * cosine],
        axis=0,
    )


def shards(traces, owners, counts, pair_table, anterp, interp, phase):
    blocks = traces[0, 0]
    destination = owners[0, 0, :, 0]
    live_count = counts[0, 0]
    param_count = lax.axis_size("param")
    slot_count = pair_table.shape[3]
    block_count = blocks.shape[0]
    trace_count = blocks.shape[1]
    weight_count = interp.shape[2]
    pair_count = phase.shape[3]
    live_mask = (jnp.arange(block_count, dtype=jnp.int32) < live_count).astype(jnp.float32)
    onehot = (destination[:, None] == jnp.arange(param_count, dtype=jnp.int32)[None, :]).astype(
        jnp.int32
    )
    ranking = jnp.sum((jnp.cumsum(onehot, axis=0) - onehot) * onehot, axis=1)
    position = destination * slot_count + ranking
    masked = blocks * live_mask[:, None]
    pair_ids = pair_table[0, 0].reshape(-1)
    selector = (jnp.arange(pair_count, dtype=jnp.int32)[:, None] == pair_ids[None, :]).astype(
        jnp.float32
    )
    outgoing = (
        jnp.zeros((param_count * slot_count, trace_count), jnp.float32).at[position].set(masked)
    )
    arrived = lax.all_to_all(
        outgoing.reshape(param_count, slot_count, trace_count),
        "param",
        split_axis=0,
        concat_axis=0,
        tiled=True,
    )
    angles = phase[0, 0]
    arrived, cosines, sines = lax.optimization_barrier((arrived, jnp.cos(angles), jnp.sin(angles)))
    gathered = jnp.dot(selector, arrived.reshape(-1, trace_count), precision=HIGH)
    weights_now = jnp.einsum(
        "pt,trk->rpk", gathered, anterp.reshape(trace_count, 2, weight_count), precision=HIGH
    )
    half_rows = pair_count // 2
    edges = [sum(CHUNK_ROWS[:i]) * half_rows // 256 for i in range(CHUNKS + 1)]
    cosines = cosines.reshape(LEVELS, 2, half_rows, weight_count)
    sines = sines.reshape(LEVELS, 2, half_rows, weight_count)
    weights_now = weights_now.reshape(2, 2, half_rows, weight_count)
    box_index = lax.axis_index("box")
    pieces = [weights_now[:, :, edges[i]:edges[i + 1]] for i in range(CHUNKS)]
    for level_id in range(LEVELS):
        side_bit = box_index >> level_id & 1
        for i in range(CHUNKS):
            piece = pieces[i]
            kept_rows = lax.dynamic_index_in_dim(piece, side_bit, 1, keepdims=False)
            sent_rows = lax.dynamic_index_in_dim(piece, 1 - side_bit, 1, keepdims=False)
            partner = swapped(sent_rows, "box", level_id)
            lower_rows = jnp.where(side_bit == 0, kept_rows, partner)
            upper_rows = jnp.where(side_bit == 0, partner, kept_rows)
            joined = jnp.concatenate([lower_rows, upper_rows], axis=2)
            combined = jnp.einsum("rqk,skj->rsqj", joined, interp, precision=HIGH)
            rows = slice(edges[i], edges[i + 1])
            pieces[i] = rotate(combined, cosines[level_id][:, rows], sines[level_id][:, rows])
    weights_now = jnp.concatenate(pieces, axis=2).reshape(2, pair_count, weight_count)
    return weights_now[None, None]


def solution(mesh):
    placed = (
        P("box", "param", None, None),
        P("box", "param", None, None),
        P("box", "param"),
        P("box", "param", None, None),
        P(),
        P(),
        P("box", "param", None, None, None),
    )
    return jax.shard_map(
        shards,
        mesh=mesh,
        in_specs=placed,
        out_specs=P("box", "param", None, None, None),
        check_vma=False,
    )
```

profile of v0, /device:TPU:258, one launch (start us, length us, event | category | flops | bytes accessed | tf_op | source)
XLA Modules:
  0.0 112.6 jit_solution(8534285203206933793)
XLA Ops:
  0.0 0.0 copy-start
  0.8 0.7 fusion.80
  1.4 1.2 %reduce-window.6 = s32[32,4,128]{2,0,1:T(8,128)S(1)} reduce-window(s32[32,4,128]{2,0,1:T(8,128)S(1)} %fusion.80, s32[]{:T(128)} %constant.77.clone.1), window={size=1x1x128 pad=0_0x0_0x127_0}, to_apply=%region_0.0 | reduce-window | flops 2080768 | bytes 131076 | tf_op jit(solution)/shard_map/reduce-window
  2.6 0.2 slice_reduce_fusion
  2.9 0.8 fusion.79
  3.7 0.7 compare_select_fusion
  4.3 0.0 copy-start.3
  4.4 3.8 %scatter_custom_fusion = f32[1024,256]{1,0:T(8,128)} fusion(s32[512]{0:T(512)S(1)} %bitcast.476, f32[1,1,512,256]{3,2,1,0:T(8,128)} %param.7, f32[]{:T(128)} %constant.78.clone.1, f32[512]{0:T(512)S(1)} %fusion.81), kind=kCustom, calls=%fused_computation.36 | custom fusion | flops 131072 | bytes 1574916 | tf_op jit(solution)/shard_map/scatter | solution.py:50
  8.2 12.1 %all-to-all-start = ((f32[32,32,256]{2,1,0:T(8,128)}), f32[32,32,256]{2,1,0:T(8,128)}, u32[]{:S(2)}, u32[]{:S(2)}) async-start(f32[32,32,256]{2,1,0:T(8,128)} %bitcast.8), calls=%async_computation | async-start | bytes 2097152 | tf_op jit(solution)/shard_map/all_to_all | solution.py:52
  20.3 0.0 copy-done.3
  20.3 0.1 eq.36
  20.4 8.2 %sine_bitcast_fusion = (f32[3,512,256]{2,1,0:T(8,128)S(1)}, f32[3,512,256]{2,1,0:T(8,128)}) fusion(f32[1,1,3,512,256]{4,3,2,1,0:T(8,128)} %param.13), kind=kLoop, calls=%fused_computation.3 | loop fusion | bytes 4718592 | tf_op jit(solution)/shard_map/sin | solution.py:60
  28.6 0.0 copy-start.2
  28.6 26.3 %all-to-all-done = f32[32,32,256]{2,1,0:T(8,128)} async-done(((f32[32,32,256]{2,1,0:T(8,128)}), f32[32,32,256]{2,1,0:T(8,128)}, u32[]{:S(2)}, u32[]{:S(2)}) %all-to-all-start) | async-done | bytes 1048608 | tf_op jit(solution)/shard_map/all_to_all | solution.py:52
  54.8 2.5 %fusion.1 = f32[512,256,1]{1,0,2:T(8,128)S(1)} fusion(f32[1024,256]{1,0:T(8,128)} %bitcast.11, s32[1024]{0:T(1024)S(1)} %eq.36), kind=kOutput, calls=%fused_computation.5 | convolution fusion | flops 1611137024 | bytes 1576960 | tf_op jit(solution)/shard_map/dot_general | solution.py:61
  57.3 0.0 copy-done.2
  57.3 1.0 fusion.15
  58.3 0.0 copy-start.1
  58.5 2.1 %collective-permute-start = (f32[2,48,256]{2,1,0:T(8,128)S(1)}, f32[2,48,256]{2,1,0:T(8,128)S(1)}, u32[]{:S(2)}, u32[]{:S(2)}) collective-permute-start(f32[2,48,256]{2,1,0:T(8,128)S(1)} %dynamic-slice_bitcast_fusion.3), channel_id=1, source_target_pairs={{0,32},{32,0},{64,96},{96,64},{128,160},{160,128},{192,224},{224,1... | collective-permute-start | bytes 294920 | tf_op jit(solution)/shard_map/ppermute | solution.py:16
  60.5 3.9 %collective-permute-start.9 = (f32[2,56,256]{2,1,0:T(8,128)S(1)}, f32[2,56,256]{2,1,0:T(8,128)S(1)}, u32[]{:S(2)}, u32[]{:S(2)}) collective-permute-start(f32[2,56,256]{2,1,0:T(8,128)S(1)} %dynamic-slice_bitcast_fusion.2), channel_id=1, source_target_pairs={{0,32},{32,0},{64,96},{96,64},{128,160},{160,128},{192,224},{224,1... | collective-permute-start | bytes 344072 | tf_op jit(solution)/shard_map/ppermute | solution.py:16
  64.5 1.9 %collective-permute-start.3 = (f32[2,72,256]{2,1,0:T(8,128)S(1)}, f32[2,72,256]{2,1,0:T(8,128)S(1)}, u32[]{:S(2)}, u32[]{:S(2)}) collective-permute-start(f32[2,72,256]{2,1,0:T(8,128)S(1)} %dynamic-slice_bitcast_fusion.1), channel_id=1, source_target_pairs={{0,32},{32,0},{64,96},{96,64},{128,160},{160,128},{192,224},{224,1... | collective-permute-start | bytes 442376 | tf_op jit(solution)/shard_map/ppermute | solution.py:16
  66.5 3.9 %collective-permute-start.6 = (f32[2,80,256]{2,1,0:T(8,128)S(1)}, f32[2,80,256]{2,1,0:T(8,128)S(1)}, u32[]{:S(2)}, u32[]{:S(2)}) collective-permute-start(f32[2,80,256]{2,1,0:T(8,128)S(1)} %dynamic-slice_bitcast_fusion), channel_id=1, source_target_pairs={{0,32},{32,0},{64,96},{96,64},{128,160},{160,128},{192,224},{224,1... | collective-permute-start | bytes 491528 | tf_op jit(solution)/shard_map/ppermute | solution.py:16
  70.4 0.0 copy-done.1
  70.4 0.3 fusion.94
  70.7 0.0 collective-permute-done
  70.8 0.0 copy-done
  70.8 0.7 convolution_bitcast_fusion.11
  71.6 1.9 %collective-permute-start.1 = (f32[2,48,256]{2,1,0:T(8,128)S(1)}, f32[2,48,256]{2,1,0:T(8,128)S(1)}, u32[]{:S(2)}, u32[]{:S(2)}) collective-permute-start(f32[2,48,256]{2,1,0:T(8,128)S(1)} %fusion.74), channel_id=1, source_target_pairs={{0,64},{32,96},{64,0},{96,32},{128,192},{160,224},{192,128},{224,1... | collective-permute-start | bytes 294920 | tf_op jit(solution)/shard_map/ppermute | solution.py:16
  73.5 0.0 collective-permute-done.9
  73.6 0.7 convolution_bitcast_fusion.8
  74.3 4.8 %collective-permute-start.10 = (f32[2,56,256]{2,1,0:T(8,128)S(1)}, f32[2,56,256]{2,1,0:T(8,128)S(1)}, u32[]{:S(2)}, u32[]{:S(2)}) collective-permute-start(f32[2,56,256]{2,1,0:T(8,128)S(1)} %fusion.66), channel_id=1, source_target_pairs={{0,64},{32,96},{64,0},{96,32},{128,192},{160,224},{192,128},{224,1... | collective-permute-start | bytes 344072 | tf_op jit(solution)/shard_map/ppermute | solution.py:16
  79.2 0.0 collective-permute-done.3
  79.2 0.8 convolution_bitcast_fusion.5
  80.0 1.9 %collective-permute-start.4 = (f32[2,72,256]{2,1,0:T(8,128)S(1)}, f32[2,72,256]{2,1,0:T(8,128)S(1)}, u32[]{:S(2)}, u32[]{:S(2)}) collective-permute-start(f32[2,72,256]{2,1,0:T(8,128)S(1)} %fusion.58), channel_id=1, source_target_pairs={{0,64},{32,96},{64,0},{96,32},{128,192},{160,224},{192,128},{224,1... | collective-permute-start | bytes 442376 | tf_op jit(solution)/shard_map/ppermute | solution.py:16
  82.0 0.0 collective-permute-done.6
  82.0 0.8 convolution_bitcast_fusion.2
  82.8 0.1 add_bitcast_fusion.2
  82.9 4.8 %collective-permute-start.7 = (f32[2,80,256]{2,1,0:T(8,128)S(1)}, f32[2,80,256]{2,1,0:T(8,128)S(1)}, u32[]{:S(2)}, u32[]{:S(2)}) collective-permute-start(f32[2,80,256]{2,1,0:T(8,128)S(1)} %fusion.50), channel_id=1, source_target_pairs={{0,64},{32,96},{64,0},{96,32},{128,192},{160,224},{192,128},{224,1... | collective-permute-start | bytes 491528 | tf_op jit(solution)/shard_map/ppermute | solution.py:16
  87.8 0.0 collective-permute-done.1
  87.8 0.7 convolution_bitcast_fusion.10
  88.6 5.2 %collective-permute-start.2 = (f32[2,48,256]{2,1,0:T(8,128)S(1)}, f32[2,48,256]{2,1,0:T(8,128)S(1)}, u32[]{:S(2)}, u32[]{:S(2)}) collective-permute-start(f32[2,48,256]{2,1,0:T(8,128)S(1)} %fusion.70), channel_id=1, source_target_pairs={{0,128},{32,160},{64,192},{96,224},{128,0},{160,32},{192,64},{224,... | collective-permute-start | bytes 294920 | tf_op jit(solution)/shard_map/ppermute | solution.py:16
  93.8 0.0 collective-permute-done.10
  93.9 0.7 convolution_bitcast_fusion.7
  94.7 2.1 %collective-permute-start.11 = (f32[2,56,256]{2,1,0:T(8,128)S(1)}, f32[2,56,256]{2,1,0:T(8,128)S(1)}, u32[]{:S(2)}, u32[]{:S(2)}) collective-permute-start(f32[2,56,256]{2,1,0:T(8,128)S(1)} %fusion.62), channel_id=1, source_target_pairs={{0,128},{32,160},{64,192},{96,224},{128,0},{160,32},{192,64},{224,... | collective-permute-start | bytes 344072 | tf_op jit(solution)/shard_map/ppermute | solution.py:16
  96.8 0.0 collective-permute-done.4
  96.8 0.7 convolution_bitcast_fusion.4
  97.7 3.9 %collective-permute-start.5 = (f32[2,72,256]{2,1,0:T(8,128)S(1)}, f32[2,72,256]{2,1,0:T(8,128)S(1)}, u32[]{:S(2)}, u32[]{:S(2)}) collective-permute-start(f32[2,72,256]{2,1,0:T(8,128)S(1)} %fusion.54), channel_id=1, source_target_pairs={{0,128},{32,160},{64,192},{96,224},{128,0},{160,32},{192,64},{224,... | collective-permute-start | bytes 442376 | tf_op jit(solution)/shard_map/ppermute | solution.py:16
  101.6 0.0 collective-permute-done.2
  101.6 0.7 convolution_bitcast_fusion.9
  102.4 0.0 collective-permute-done.7
  102.5 0.8 convolution_bitcast_fusion.1
  103.3 0.1 add_bitcast_fusion.1
  103.4 1.9 %collective-permute-start.8 = (f32[2,80,256]{2,1,0:T(8,128)S(1)}, f32[2,80,256]{2,1,0:T(8,128)S(1)}, u32[]{:S(2)}, u32[]{:S(2)}) collective-permute-start(f32[2,80,256]{2,1,0:T(8,128)S(1)} %fusion.46), channel_id=1, source_target_pairs={{0,128},{32,160},{64,192},{96,224},{128,0},{160,32},{192,64},{224,... | collective-permute-start | bytes 491528 | tf_op jit(solution)/shard_map/ppermute | solution.py:16
  105.3 0.0 collective-permute-done.11
  105.3 0.7 convolution_bitcast_fusion.6
  106.1 0.0 collective-permute-done.5
  106.2 0.7 convolution_bitcast_fusion.3
  107.0 3.6 %collective-permute-done.8 = f32[2,80,256]{2,1,0:T(8,128)S(1)} collective-permute-done((f32[2,80,256]{2,1,0:T(8,128)S(1)}, f32[2,80,256]{2,1,0:T(8,128)S(1)}, u32[]{:S(2)}, u32[]{:S(2)}) %collective-permute-start.8) | collective-permute-done | bytes 163872 | tf_op jit(solution)/shard_map/ppermute | solution.py:16
  110.6 0.8 convolution_bitcast_fusion
  111.4 0.1 subtract_bitcast_fusion
  111.5 1.0 maximum_maximum_fusion
  (40 shorter events, 1.0 us)
Async XLA Ops:
  0.0 70.8 %copy-start = (f32[2,512,256]{2,1,0:T(8,128)S(1)}, f32[2,512,256]{2,1,0:T(8,128)}, u32[]{:S(2)}) copy-start(f32[2,512,256]{2,1,0:T(8,128)} %param.12) | copy-start | bytes 3145732
  4.3 16.0 %copy-start.3 = (s32[1,1,32,32]{3,2,1,0:T(8,128)S(1)}, s32[1,1,32,32]{3,2,1,0:T(8,128)}, u32[]{:S(2)}) copy-start(s32[1,1,32,32]{3,2,1,0:T(8,128)} %param.10) | copy-start | bytes 12292
  8.2 46.6 %all-to-all-start = ((f32[32,32,256]{2,1,0:T(8,128)}), f32[32,32,256]{2,1,0:T(8,128)}, u32[]{:S(2)}, u32[]{:S(2)}) async-start(f32[32,32,256]{2,1,0:T(8,128)} %bitcast.8), calls=%async_computation | async-start | bytes 2097152 | tf_op jit(solution)/shard_map/all_to_all | solution.py:52
  28.6 28.7 %copy-start.2 = (f32[256,512]{1,0:T(8,128)S(1)}, f32[256,512]{1,0:T(8,128)}, u32[]{:S(2)}) copy-start(f32[256,512]{1,0:T(8,128)} %param.11) | copy-start | bytes 1572868
  58.3 12.1 %copy-start.1 = (f32[3,512,256]{2,1,0:T(8,128)S(1)}, f32[3,512,256]{2,1,0:T(8,128)}, u32[]{:S(2)}) copy-start(f32[3,512,256]{2,1,0:T(8,128)} %get-tuple-element.9) | copy-start | bytes 4718596
  58.5 12.3 %collective-permute-start = (f32[2,48,256]{2,1,0:T(8,128)S(1)}, f32[2,48,256]{2,1,0:T(8,128)S(1)}, u32[]{:S(2)}, u32[]{:S(2)}) collective-permute-start(f32[2,48,256]{2,1,0:T(8,128)S(1)} %dynamic-slice_bitcast_fusion.3), channel_id=1, source_target_pairs={{0,32},{32,0},{64,96},{96,64},{128,160},{160,128},{192,224},{224,1... | collective-permute-start | bytes 294920 | tf_op jit(solution)/shard_map/ppermute | solution.py:16
  60.5 13.0 %collective-permute-start.9 = (f32[2,56,256]{2,1,0:T(8,128)S(1)}, f32[2,56,256]{2,1,0:T(8,128)S(1)}, u32[]{:S(2)}, u32[]{:S(2)}) collective-permute-start(f32[2,56,256]{2,1,0:T(8,128)S(1)} %dynamic-slice_bitcast_fusion.2), channel_id=1, source_target_pairs={{0,32},{32,0},{64,96},{96,64},{128,160},{160,128},{192,224},{224,1... | collective-permute-start | bytes 344072 | tf_op jit(solution)/shard_map/ppermute | solution.py:16
  64.5 14.7 %collective-permute-start.3 = (f32[2,72,256]{2,1,0:T(8,128)S(1)}, f32[2,72,256]{2,1,0:T(8,128)S(1)}, u32[]{:S(2)}, u32[]{:S(2)}) collective-permute-start(f32[2,72,256]{2,1,0:T(8,128)S(1)} %dynamic-slice_bitcast_fusion.1), channel_id=1, source_target_pairs={{0,32},{32,0},{64,96},{96,64},{128,160},{160,128},{192,224},{224,1... | collective-permute-start | bytes 442376 | tf_op jit(solution)/shard_map/ppermute | solution.py:16
  66.5 15.5 %collective-permute-start.6 = (f32[2,80,256]{2,1,0:T(8,128)S(1)}, f32[2,80,256]{2,1,0:T(8,128)S(1)}, u32[]{:S(2)}, u32[]{:S(2)}) collective-permute-start(f32[2,80,256]{2,1,0:T(8,128)S(1)} %dynamic-slice_bitcast_fusion), channel_id=1, source_target_pairs={{0,32},{32,0},{64,96},{96,64},{128,160},{160,128},{192,224},{224,1... | collective-permute-start | bytes 491528 | tf_op jit(solution)/shard_map/ppermute | solution.py:16
  71.6 16.2 %collective-permute-start.1 = (f32[2,48,256]{2,1,0:T(8,128)S(1)}, f32[2,48,256]{2,1,0:T(8,128)S(1)}, u32[]{:S(2)}, u32[]{:S(2)}) collective-permute-start(f32[2,48,256]{2,1,0:T(8,128)S(1)} %fusion.74), channel_id=1, source_target_pairs={{0,64},{32,96},{64,0},{96,32},{128,192},{160,224},{192,128},{224,1... | collective-permute-start | bytes 294920 | tf_op jit(solution)/shard_map/ppermute | solution.py:16
  74.3 19.5 %collective-permute-start.10 = (f32[2,56,256]{2,1,0:T(8,128)S(1)}, f32[2,56,256]{2,1,0:T(8,128)S(1)}, u32[]{:S(2)}, u32[]{:S(2)}) collective-permute-start(f32[2,56,256]{2,1,0:T(8,128)S(1)} %fusion.66), channel_id=1, source_target_pairs={{0,64},{32,96},{64,0},{96,32},{128,192},{160,224},{192,128},{224,1... | collective-permute-start | bytes 344072 | tf_op jit(solution)/shard_map/ppermute | solution.py:16
  80.0 16.7 %collective-permute-start.4 = (f32[2,72,256]{2,1,0:T(8,128)S(1)}, f32[2,72,256]{2,1,0:T(8,128)S(1)}, u32[]{:S(2)}, u32[]{:S(2)}) collective-permute-start(f32[2,72,256]{2,1,0:T(8,128)S(1)} %fusion.58), channel_id=1, source_target_pairs={{0,64},{32,96},{64,0},{96,32},{128,192},{160,224},{192,128},{224,1... | collective-permute-start | bytes 442376 | tf_op jit(solution)/shard_map/ppermute | solution.py:16
  82.9 19.5 %collective-permute-start.7 = (f32[2,80,256]{2,1,0:T(8,128)S(1)}, f32[2,80,256]{2,1,0:T(8,128)S(1)}, u32[]{:S(2)}, u32[]{:S(2)}) collective-permute-start(f32[2,80,256]{2,1,0:T(8,128)S(1)} %fusion.50), channel_id=1, source_target_pairs={{0,64},{32,96},{64,0},{96,32},{128,192},{160,224},{192,128},{224,1... | collective-permute-start | bytes 491528 | tf_op jit(solution)/shard_map/ppermute | solution.py:16
  88.6 13.0 %collective-permute-start.2 = (f32[2,48,256]{2,1,0:T(8,128)S(1)}, f32[2,48,256]{2,1,0:T(8,128)S(1)}, u32[]{:S(2)}, u32[]{:S(2)}) collective-permute-start(f32[2,48,256]{2,1,0:T(8,128)S(1)} %fusion.70), channel_id=1, source_target_pairs={{0,128},{32,160},{64,192},{96,224},{128,0},{160,32},{192,64},{224,... | collective-permute-start | bytes 294920 | tf_op jit(solution)/shard_map/ppermute | solution.py:16
  94.7 10.6 %collective-permute-start.11 = (f32[2,56,256]{2,1,0:T(8,128)S(1)}, f32[2,56,256]{2,1,0:T(8,128)S(1)}, u32[]{:S(2)}, u32[]{:S(2)}) collective-permute-start(f32[2,56,256]{2,1,0:T(8,128)S(1)} %fusion.62), channel_id=1, source_target_pairs={{0,128},{32,160},{64,192},{96,224},{128,0},{160,32},{192,64},{224,... | collective-permute-start | bytes 344072 | tf_op jit(solution)/shard_map/ppermute | solution.py:16
  97.7 8.5 %collective-permute-start.5 = (f32[2,72,256]{2,1,0:T(8,128)S(1)}, f32[2,72,256]{2,1,0:T(8,128)S(1)}, u32[]{:S(2)}, u32[]{:S(2)}) collective-permute-start(f32[2,72,256]{2,1,0:T(8,128)S(1)} %fusion.54), channel_id=1, source_target_pairs={{0,128},{32,160},{64,192},{96,224},{128,0},{160,32},{192,64},{224,... | collective-permute-start | bytes 442376 | tf_op jit(solution)/shard_map/ppermute | solution.py:16
  103.4 7.2 %collective-permute-start.8 = (f32[2,80,256]{2,1,0:T(8,128)S(1)}, f32[2,80,256]{2,1,0:T(8,128)S(1)}, u32[]{:S(2)}, u32[]{:S(2)}) collective-permute-start(f32[2,80,256]{2,1,0:T(8,128)S(1)} %fusion.46), channel_id=1, source_target_pairs={{0,128},{32,160},{64,192},{96,224},{128,0},{160,32},{192,64},{224,... | collective-permute-start | bytes 491528 | tf_op jit(solution)/shard_map/ppermute | solution.py:16
where the time goes:
time: 113 us
  starting transfers between devices  50.6 us (45%)
  waiting for transfers between devices  29.9 us (26%)
  matrix products  12.4 us (11%)
  other arithmetic  9.35 us (8%)
  local copies, waits for them, and re-layouts  8.95 us (8%)
  between operations  1.35 us (1%)
    ppermute x12, starting transfers between devices, swapped(): lax.ppermute(x, axis, [(i, i ^ 1 << bit) for i in range(lax.axis_size(axi...  38.5 us
    all_to_all x1, waiting for transfers between devices, shards(): lax.all_to_all(outgoing.reshape(param_count, slot_count, trace_count), 'p...  26.3 us
    all_to_all x1, starting transfers between devices, shards(): lax.all_to_all(outgoing.reshape(param_count, slot_count, trace_count), 'p...  12.1 us
    dot_general x12, matrix products, shards(): combined = jnp.einsum('rqk,skj->rsqj', joined, interp, precision=HIGH)  8.97 us
    sin x1, local copies, waits for them, and re-layouts, shards(): jnp.sin(angles)  8.16 us
    scatter x1, other arithmetic, shards(): jnp.zeros((param_count * slot_count, trace_count), jnp.float32).at[position]  3.85 us
    ppermute x12, waiting for transfers between devices, swapped(): lax.ppermute(x, axis, [(i, i ^ 1 << bit) for i in range(lax.axis_size(axi...  3.66 us
    dot_general x1, matrix products, shards(): jnp.dot(selector, arrived.reshape(-1, trace_count), precision=HIGH)  2.46 us
  transfers between devices with their start and end apart: 13, of which 2 were waited for; matrix products, arithmetic and copies ran while one was open for 16% of the time, Pallas kernels for 0%

commit v1 on v0

--- a/solution.py
+++ b/solution.py
@@ -5,7 +5,7 @@
 
 
 LEVELS = 3
-CHUNK_ROWS = (48, 72, 80, 56)
+CHUNK_ROWS = (120, 136)
 CHUNKS = len(CHUNK_ROWS)
 
 
@@ -35,20 +35,22 @@
     trace_count = blocks.shape[1]
     weight_count = interp.shape[2]
     pair_count = phase.shape[3]
-    live_mask = (jnp.arange(block_count, dtype=jnp.int32) < live_count).astype(jnp.float32)
+    row_ids = jnp.arange(block_count, dtype=jnp.int32)
+    live_mask = (row_ids < live_count).astype(jnp.float32)
     onehot = (destination[:, None] == jnp.arange(param_count, dtype=jnp.int32)[None, :]).astype(
-        jnp.int32
+        jnp.float32
     )
-    ranking = jnp.sum((jnp.cumsum(onehot, axis=0) - onehot) * onehot, axis=1)
+    earlier = (row_ids[None, :] < row_ids[:, None]).astype(jnp.float32)
+    prior = jnp.dot(earlier, onehot, preferred_element_type=jnp.float32)
+    ranking = jnp.sum(prior * onehot, axis=1).astype(jnp.int32)
     position = destination * slot_count + ranking
-    masked = blocks * live_mask[:, None]
     pair_ids = pair_table[0, 0].reshape(-1)
     selector = (jnp.arange(pair_count, dtype=jnp.int32)[:, None] == pair_ids[None, :]).astype(
         jnp.float32
     )
-    outgoing = (
-        jnp.zeros((param_count * slot_count, trace_count), jnp.float32).at[position].set(masked)
-    )
+    slots = jnp.arange(param_count * slot_count, dtype=jnp.int32)
+    placement = jnp.where(slots[:, None] == position[None, :], live_mask[None, :], 0.0)
+    outgoing = jnp.dot(placement, blocks, precision=HIGH)
     arrived = lax.all_to_all(
         outgoing.reshape(param_count, slot_count, trace_count),
         "param",

time: 113 us -> 107 us (0.947)
  the two profiles are of different devices: /device:TPU:258 before, /device:TPU:32 now
where the time goes in v1:
time: 107 us
  waiting for transfers between devices  44.4 us (41%)
  starting transfers between devices  35 us (33%)
  matrix products  14.7 us (14%)
  local copies, waits for them, and re-layouts  8.68 us (8%)
  other arithmetic  2.78 us (3%)
    ppermute x6, waiting for transfers between devices, swapped(): lax.ppermute(x, axis, [(i, i ^ 1 << bit) for i in range(lax.axis_size(axi...  24.5 us
    all_to_all x1, waiting for transfers between devices, shards(): lax.all_to_all(outgoing.reshape(param_count, slot_count, trace_count), 'p...  19.9 us
    ppermute x6, starting transfers between devices, swapped(): lax.ppermute(x, axis, [(i, i ^ 1 << bit) for i in range(lax.axis_size(axi...  17.9 us
    all_to_all x1, starting transfers between devices, shards(): lax.all_to_all(outgoing.reshape(param_count, slot_count, trace_count), 'p...  17.2 us
    sin x1, local copies, waits for them, and re-layouts, shards(): jnp.sin(angles)  8.14 us
    dot_general x6, matrix products, shards(): combined = jnp.einsum('rqk,skj->rsqj', joined, interp, precision=HIGH)  6.32 us
    dot_general x1, matrix products, shards(): outgoing = jnp.dot(placement, blocks, precision=HIGH)  3.86 us
    dot_general x1, matrix products, shards(): jnp.dot(selector, arrived.reshape(-1, trace_count), precision=HIGH)  2.45 us
  transfers between devices with their start and end apart: 7, of which 6 were waited for; matrix products, arithmetic and copies ran while one was open for 14% of the time, Pallas kernels for 0%

profile of v1, /device:TPU:32, one launch (start us, length us, event | category | flops | bytes accessed | tf_op | source)
XLA Modules:
  0.0 106.7 jit_solution(950068441439923143)
XLA Ops:
  0.0 0.0 copy-start
  0.8 1.0 fusion.5
  1.8 0.7 convert_add_fusion
  2.5 3.9 %fusion = f32[32,32,256]{2,1,0:T(8,128)} fusion(f32[512]{0:T(512)S(1)} %fusion.50, s32[512]{0:T(512)S(1)} %convert_add_fusion, s32[32,32]{1,0:T(8,128)S(1)} %multiply_add_fusion, f32[1,1,512,256]{3,2,1,0:T(8,128)} %param.7), kind=kOutput, calls=%fused_computation | convolution fusion | flops 1611661312 | bytes 1581056 | tf_op jit(solution)/shard_map/dot_general | solution.py:53
  6.3 0.0 copy-start.3
  6.3 17.2 %all-to-all-start = ((f32[32,32,256]{2,1,0:T(8,128)}), f32[32,32,256]{2,1,0:T(8,128)}, u32[]{:S(2)}, u32[]{:S(2)}) async-start(f32[32,32,256]{2,1,0:T(8,128)} %fusion), calls=%async_computation | async-start | bytes 2097152 | tf_op jit(solution)/shard_map/all_to_all | solution.py:54
  23.5 0.0 copy-done.3
  23.5 0.1 eq.74
  23.6 8.1 %sine_bitcast_fusion = (f32[3,512,256]{2,1,0:T(8,128)S(1)}, f32[3,512,256]{2,1,0:T(8,128)}) fusion(f32[1,1,3,512,256]{4,3,2,1,0:T(8,128)} %param.13), kind=kLoop, calls=%fused_computation.5 | loop fusion | bytes 4718592 | tf_op jit(solution)/shard_map/sin | solution.py:62
  31.7 0.0 copy-start.2
  31.7 19.9 %all-to-all-done = f32[32,32,256]{2,1,0:T(8,128)} async-done(((f32[32,32,256]{2,1,0:T(8,128)}), f32[32,32,256]{2,1,0:T(8,128)}, u32[]{:S(2)}, u32[]{:S(2)}) %all-to-all-start) | async-done | bytes 1048608 | tf_op jit(solution)/shard_map/all_to_all | solution.py:54
  51.6 2.5 %fusion.4 = f32[512,256,1]{1,0,2:T(8,128)S(1)} fusion(f32[1024,256]{1,0:T(8,128)} %bitcast.6, s32[1024]{0:T(1024)S(1)} %eq.74), kind=kOutput, calls=%fused_computation.10 | convolution fusion | flops 1611137024 | bytes 1576960 | tf_op jit(solution)/shard_map/dot_general | solution.py:63
  54.1 0.0 copy-done.2
  54.1 1.0 fusion.23
  55.1 0.0 copy-start.1
  55.3 4.7 %collective-permute-start = (f32[2,120,256]{2,1,0:T(8,128)S(1)}, f32[2,120,256]{2,1,0:T(8,128)S(1)}, u32[]{:S(2)}, u32[]{:S(2)}) collective-permute-start(f32[2,120,256]{2,1,0:T(8,128)S(1)} %dynamic-slice_bitcast_fusion.1), channel_id=1, source_target_pairs={{0,32},{32,0},{64,96},{96,64},{128,160},{160,128},{192,224},{224,1... | collective-permute-start | bytes 737288 | tf_op jit(solution)/shard_map/ppermute | solution.py:16
  60.0 1.9 %collective-permute-start.3 = (f32[2,136,256]{2,1,0:T(8,128)S(1)}, f32[2,136,256]{2,1,0:T(8,128)S(1)}, u32[]{:S(2)}, u32[]{:S(2)}) collective-permute-start(f32[2,136,256]{2,1,0:T(8,128)S(1)} %dynamic-slice_bitcast_fusion), channel_id=1, source_target_pairs={{0,32},{32,0},{64,96},{96,64},{128,160},{160,128},{192,224},{224,1... | collective-permute-start | bytes 835592 | tf_op jit(solution)/shard_map/ppermute | solution.py:16
  62.0 0.0 copy-done.1
  62.0 0.3 fusion.58
  62.3 4.3 %collective-permute-done = f32[2,120,256]{2,1,0:T(8,128)S(1)} collective-permute-done((f32[2,120,256]{2,1,0:T(8,128)S(1)}, f32[2,120,256]{2,1,0:T(8,128)S(1)}, u32[]{:S(2)}, u32[]{:S(2)}) %collective-permute-start) | collective-permute-done | bytes 245792 | tf_op jit(solution)/shard_map/ppermute | solution.py:16
  66.7 0.0 copy-done
  66.7 1.0 convolution_bitcast_fusion.5
  67.7 0.1 add_bitcast_fusion.5
  67.8 1.9 %collective-permute-start.1 = (f32[2,120,256]{2,1,0:T(8,128)S(1)}, f32[2,120,256]{2,1,0:T(8,128)S(1)}, u32[]{:S(2)}, u32[]{:S(2)}) collective-permute-start(f32[2,120,256]{2,1,0:T(8,128)S(1)} %fusion.46), channel_id=1, source_target_pairs={{0,64},{32,96},{64,0},{96,32},{128,192},{160,224},{192,128},{224,1... | collective-permute-start | bytes 737288 | tf_op jit(solution)/shard_map/ppermute | solution.py:16
  69.7 3.0 %collective-permute-done.3 = f32[2,136,256]{2,1,0:T(8,128)S(1)} collective-permute-done((f32[2,136,256]{2,1,0:T(8,128)S(1)}, f32[2,136,256]{2,1,0:T(8,128)S(1)}, u32[]{:S(2)}, u32[]{:S(2)}) %collective-permute-start.3) | collective-permute-done | bytes 278560 | tf_op jit(solution)/shard_map/ppermute | solution.py:16
  72.8 1.1 %convolution_bitcast_fusion.2 = f32[2,2,136,256]{3,2,1,0:T(8,128)S(1)} fusion(f32[2,512,256]{2,1,0:T(8,128)S(1)} %copy-done, f32[2,136,256]{2,1,0:T(8,128)S(1)} %get-tuple-element.36, f32[2,136,256]{2,1,0:T(8,128)S(1)} %get-tuple-element.35), kind=kOutput, calls=%fused_computation.9 | convolution fusion | flops 855777280 | bytes 2162688 | tf_op jit(solution)/shard_map/rqk,skj->rsqj/dot_general | solution.py:84
  73.9 0.1 add_bitcast_fusion.2
  74.1 1.9 %collective-permute-start.4 = (f32[2,136,256]{2,1,0:T(8,128)S(1)}, f32[2,136,256]{2,1,0:T(8,128)S(1)}, u32[]{:S(2)}, u32[]{:S(2)}) collective-permute-start(f32[2,136,256]{2,1,0:T(8,128)S(1)} %fusion.38), channel_id=1, source_target_pairs={{0,64},{32,96},{64,0},{96,32},{128,192},{160,224},{192,128},{224,1... | collective-permute-start | bytes 835592 | tf_op jit(solution)/shard_map/ppermute | solution.py:16
  76.0 11.8 %collective-permute-done.1 = f32[2,120,256]{2,1,0:T(8,128)S(1)} collective-permute-done((f32[2,120,256]{2,1,0:T(8,128)S(1)}, f32[2,120,256]{2,1,0:T(8,128)S(1)}, u32[]{:S(2)}, u32[]{:S(2)}) %collective-permute-start.1) | collective-permute-done | bytes 245792 | tf_op jit(solution)/shard_map/ppermute | solution.py:16
  87.8 1.0 convolution_bitcast_fusion.4
  88.9 0.1 add_bitcast_fusion.4
  89.0 5.2 %collective-permute-start.2 = (f32[2,120,256]{2,1,0:T(8,128)S(1)}, f32[2,120,256]{2,1,0:T(8,128)S(1)}, u32[]{:S(2)}, u32[]{:S(2)}) collective-permute-start(f32[2,120,256]{2,1,0:T(8,128)S(1)} %fusion.42), channel_id=1, source_target_pairs={{0,128},{32,160},{64,192},{96,224},{128,0},{160,32},{192,64},{224,... | collective-permute-start | bytes 737288 | tf_op jit(solution)/shard_map/ppermute | solution.py:16
  94.2 0.0 collective-permute-done.4
  94.2 0.1 broadcast_select_fusion.1
  94.3 1.1 %convolution_bitcast_fusion.1 = f32[2,2,136,256]{3,2,1,0:T(8,128)S(1)} fusion(f32[2,512,256]{2,1,0:T(8,128)S(1)} %copy-done, f32[2,136,256]{2,1,0:T(8,128)S(1)} %get-tuple-element.34, f32[2,136,256]{2,1,0:T(8,128)S(1)} %get-tuple-element.33), kind=kOutput, calls=%fused_computation.8 | convolution fusion | flops 855777280 | bytes 2162688 | tf_op jit(solution)/shard_map/rqk,skj->rsqj/dot_general | solution.py:84
  95.4 0.1 add_bitcast_fusion.1
  95.5 2.2 %collective-permute-start.5 = (f32[2,136,256]{2,1,0:T(8,128)S(1)}, f32[2,136,256]{2,1,0:T(8,128)S(1)}, u32[]{:S(2)}, u32[]{:S(2)}) collective-permute-start(f32[2,136,256]{2,1,0:T(8,128)S(1)} %fusion.34), channel_id=1, source_target_pairs={{0,128},{32,160},{64,192},{96,224},{128,0},{160,32},{192,64},{224,... | collective-permute-start | bytes 835592 | tf_op jit(solution)/shard_map/ppermute | solution.py:16
  97.8 2.8 %collective-permute-done.2 = f32[2,120,256]{2,1,0:T(8,128)S(1)} collective-permute-done((f32[2,120,256]{2,1,0:T(8,128)S(1)}, f32[2,120,256]{2,1,0:T(8,128)S(1)}, u32[]{:S(2)}, u32[]{:S(2)}) %collective-permute-start.2) | collective-permute-done | bytes 245792 | tf_op jit(solution)/shard_map/ppermute | solution.py:16
  100.6 1.0 convolution_bitcast_fusion.3
  101.6 0.1 subtract_bitcast_fusion.3
  101.7 2.6 %collective-permute-done.5 = f32[2,136,256]{2,1,0:T(8,128)S(1)} collective-permute-done((f32[2,136,256]{2,1,0:T(8,128)S(1)}, f32[2,136,256]{2,1,0:T(8,128)S(1)}, u32[]{:S(2)}, u32[]{:S(2)}) %collective-permute-start.5) | collective-permute-done | bytes 278560 | tf_op jit(solution)/shard_map/ppermute | solution.py:16
  104.4 1.1 %convolution_bitcast_fusion = f32[2,2,136,256]{3,2,1,0:T(8,128)S(1)} fusion(f32[2,512,256]{2,1,0:T(8,128)S(1)} %copy-done, f32[2,136,256]{2,1,0:T(8,128)S(1)} %get-tuple-element.32, f32[2,136,256]{2,1,0:T(8,128)S(1)} %get-tuple-element.31), kind=kOutput, calls=%fused_computation.7 | convolution fusion | flops 855777280 | bytes 2162688 | tf_op jit(solution)/shard_map/rqk,skj->rsqj/dot_general | solution.py:84
  105.5 0.1 subtract_bitcast_fusion
  105.6 1.1 %maximum_maximum_fusion = f32[2,2,256,256]{3,2,1,0:T(8,128)} fusion(f32[1,2,136,256]{3,2,1,0:T(8,128)S(1)} %get-tuple-element.12, f32[1,2,136,256]{3,2,1,0:T(8,128)S(1)} %get-tuple-element.11, f32[1,2,120,256]{3,2,1,0:T(8,128)S(1)} %get-tuple-element.26, f32[1,2,120,256]{3,2,1,0:T(8,128)S(1)} %get-tuple-element.25), kind=kLoop, calls=%fused_computation.16 | loop fusion | flops 786432 | bytes 2097152 | tf_op jit(solution)/shard_map/concatenate | solution.py:87
  (15 shorter events, 0.5 us)
Async XLA Ops:
  0.0 66.7 %copy-start = (f32[2,512,256]{2,1,0:T(8,128)S(1)}, f32[2,512,256]{2,1,0:T(8,128)}, u32[]{:S(2)}) copy-start(f32[2,512,256]{2,1,0:T(8,128)} %param.12) | copy-start | bytes 3145732
  6.3 17.2 %copy-start.3 = (s32[1,1,32,32]{3,2,1,0:T(8,128)S(1)}, s32[1,1,32,32]{3,2,1,0:T(8,128)}, u32[]{:S(2)}) copy-start(s32[1,1,32,32]{3,2,1,0:T(8,128)} %param.10) | copy-start | bytes 12292
  6.3 45.3 %all-to-all-start = ((f32[32,32,256]{2,1,0:T(8,128)}), f32[32,32,256]{2,1,0:T(8,128)}, u32[]{:S(2)}, u32[]{:S(2)}) async-start(f32[32,32,256]{2,1,0:T(8,128)} %fusion), calls=%async_computation | async-start | bytes 2097152 | tf_op jit(solution)/shard_map/all_to_all | solution.py:54
  31.7 22.4 %copy-start.2 = (f32[256,512]{1,0:T(8,128)S(1)}, f32[256,512]{1,0:T(8,128)}, u32[]{:S(2)}) copy-start(f32[256,512]{1,0:T(8,128)} %param.11) | copy-start | bytes 1572868
  55.1 6.8 %copy-start.1 = (f32[3,512,256]{2,1,0:T(8,128)S(1)}, f32[3,512,256]{2,1,0:T(8,128)}, u32[]{:S(2)}) copy-start(f32[3,512,256]{2,1,0:T(8,128)} %get-tuple-element.9) | copy-start | bytes 4718596
  55.3 11.3 %collective-permute-start = (f32[2,120,256]{2,1,0:T(8,128)S(1)}, f32[2,120,256]{2,1,0:T(8,128)S(1)}, u32[]{:S(2)}, u32[]{:S(2)}) collective-permute-start(f32[2,120,256]{2,1,0:T(8,128)S(1)} %dynamic-slice_bitcast_fusion.1), channel_id=1, source_target_pairs={{0,32},{32,0},{64,96},{96,64},{128,160},{160,128},{192,224},{224,1... | collective-permute-start | bytes 737288 | tf_op jit(solution)/shard_map/ppermute | solution.py:16
  60.0 12.7 %collective-permute-start.3 = (f32[2,136,256]{2,1,0:T(8,128)S(1)}, f32[2,136,256]{2,1,0:T(8,128)S(1)}, u32[]{:S(2)}, u32[]{:S(2)}) collective-permute-start(f32[2,136,256]{2,1,0:T(8,128)S(1)} %dynamic-slice_bitcast_fusion), channel_id=1, source_target_pairs={{0,32},{32,0},{64,96},{96,64},{128,160},{160,128},{192,224},{224,1... | collective-permute-start | bytes 835592 | tf_op jit(solution)/shard_map/ppermute | solution.py:16
  67.8 20.0 %collective-permute-start.1 = (f32[2,120,256]{2,1,0:T(8,128)S(1)}, f32[2,120,256]{2,1,0:T(8,128)S(1)}, u32[]{:S(2)}, u32[]{:S(2)}) collective-permute-start(f32[2,120,256]{2,1,0:T(8,128)S(1)} %fusion.46), channel_id=1, source_target_pairs={{0,64},{32,96},{64,0},{96,32},{128,192},{160,224},{192,128},{224,1... | collective-permute-start | bytes 737288 | tf_op jit(solution)/shard_map/ppermute | solution.py:16
  74.1 20.1 %collective-permute-start.4 = (f32[2,136,256]{2,1,0:T(8,128)S(1)}, f32[2,136,256]{2,1,0:T(8,128)S(1)}, u32[]{:S(2)}, u32[]{:S(2)}) collective-permute-start(f32[2,136,256]{2,1,0:T(8,128)S(1)} %fusion.38), channel_id=1, source_target_pairs={{0,64},{32,96},{64,0},{96,32},{128,192},{160,224},{192,128},{224,1... | collective-permute-start | bytes 835592 | tf_op jit(solution)/shard_map/ppermute | solution.py:16
  89.0 11.6 %collective-permute-start.2 = (f32[2,120,256]{2,1,0:T(8,128)S(1)}, f32[2,120,256]{2,1,0:T(8,128)S(1)}, u32[]{:S(2)}, u32[]{:S(2)}) collective-permute-start(f32[2,120,256]{2,1,0:T(8,128)S(1)} %fusion.42), channel_id=1, source_target_pairs={{0,128},{32,160},{64,192},{96,224},{128,0},{160,32},{192,64},{224,... | collective-permute-start | bytes 737288 | tf_op jit(solution)/shard_map/ppermute | solution.py:16
  95.5 8.8 %collective-permute-start.5 = (f32[2,136,256]{2,1,0:T(8,128)S(1)}, f32[2,136,256]{2,1,0:T(8,128)S(1)}, u32[]{:S(2)}, u32[]{:S(2)}) collective-permute-start(f32[2,136,256]{2,1,0:T(8,128)S(1)} %fusion.34), channel_id=1, source_target_pairs={{0,128},{32,160},{64,192},{96,224},{128,0},{160,32},{192,64},{224,... | collective-permute-start | bytes 835592 | tf_op jit(solution)/shard_map/ppermute | solution.py:16

commit v2 on v1

--- a/solution.py
+++ b/solution.py
@@ -70,21 +70,40 @@
     sines = sines.reshape(LEVELS, 2, half_rows, weight_count)
     weights_now = weights_now.reshape(2, 2, half_rows, weight_count)
     box_index = lax.axis_index("box")
-    pieces = [weights_now[:, :, edges[i]:edges[i + 1]] for i in range(CHUNKS)]
+    bits = [box_index >> level_id & 1 for level_id in range(LEVELS)]
+    kept_parts, sent_parts = [], []
+    for i in range(CHUNKS):
+        piece = weights_now[:, :, edges[i]:edges[i + 1]]
+        kept_parts.append(lax.dynamic_index_in_dim(piece, bits[0], 1, keepdims=False))
+        sent_parts.append(lax.dynamic_index_in_dim(piece, 1 - bits[0], 1, keepdims=False))
+    outputs = [None] * CHUNKS
     for level_id in range(LEVELS):
-        side_bit = box_index >> level_id & 1
+        side_bit = bits[level_id]
+        own_map = lax.dynamic_slice_in_dim(interp, side_bit * half_rows, half_rows, 1)
+        partner_map = lax.dynamic_slice_in_dim(interp, (1 - side_bit) * half_rows, half_rows, 1)
         for i in range(CHUNKS):
-            piece = pieces[i]
-            kept_rows = lax.dynamic_index_in_dim(piece, side_bit, 1, keepdims=False)
-            sent_rows = lax.dynamic_index_in_dim(piece, 1 - side_bit, 1, keepdims=False)
-            partner = swapped(sent_rows, "box", level_id)
-            lower_rows = jnp.where(side_bit == 0, kept_rows, partner)
-            upper_rows = jnp.where(side_bit == 0, partner, kept_rows)
-            joined = jnp.concatenate([lower_rows, upper_rows], axis=2)
-            combined = jnp.einsum("rqk,skj->rsqj", joined, interp, precision=HIGH)
+            partner = swapped(sent_parts[i], "box", level_id)
+            own = jnp.einsum("rqk,skj->srqj", kept_parts[i], own_map, precision=HIGH)
             rows = slice(edges[i], edges[i + 1])
-            pieces[i] = rotate(combined, cosines[level_id][:, rows], sines[level_id][:, rows])
-    weights_now = jnp.concatenate(pieces, axis=2).reshape(2, pair_count, weight_count)
+
+            def half(s, own=own, partner=partner, rows=rows):
+                mixed = lax.dynamic_index_in_dim(own, s, 0, keepdims=False) + jnp.einsum(
+                    "rqk,kj->rqj",
+                    partner,
+                    lax.dynamic_index_in_dim(partner_map, s, 0, keepdims=False),
+                    precision=HIGH,
+                )
+                cosine = lax.dynamic_index_in_dim(cosines[level_id], s, 0, keepdims=False)[rows]
+                sine_part = lax.dynamic_index_in_dim(sines[level_id], s, 0, keepdims=False)[rows]
+                return rotate(mixed, cosine, sine_part)
+
+            if level_id + 1 < LEVELS:
+                next_bit = bits[level_id + 1]
+                sent_parts[i] = half(1 - next_bit)
+                kept_parts[i] = half(next_bit)
+            else:
+                outputs[i] = jnp.stack([half(0), half(1)], axis=1)
+    weights_now = jnp.concatenate(outputs, axis=2).reshape(2, pair_count, weight_count)
     return weights_now[None, None]
 
 

time: 107 us -> 108 us (level)
  the two profiles are of different devices: /device:TPU:32 before, /device:TPU:256 now
where the time goes in v2:
time: 108 us; the launch traced here: 107 us
  waiting for transfers between devices  42.9 us (40%)
  starting transfers between devices  35.1 us (32%)
  matrix products  17 us (16%)
  local copies, waits for them, and re-layouts  9.54 us (9%)
  other arithmetic  1.54 us (1%)
  between operations  1.13 us (1%)
    ppermute x6, starting transfers between devices, swapped(): lax.ppermute(x, axis, [(i, i ^ 1 << bit) for i in range(lax.axis_size(axi...  21.9 us
    ppermute x6, waiting for transfers between devices, swapped(): lax.ppermute(x, axis, [(i, i ^ 1 << bit) for i in range(lax.axis_size(axi...  21.7 us
    all_to_all x1, waiting for transfers between devices, shards(): lax.all_to_all(outgoing.reshape(param_count, slot_count, trace_count), 'p...  21.2 us
    all_to_all x1, starting transfers between devices, shards(): lax.all_to_all(outgoing.reshape(param_count, slot_count, trace_count), 'p...  13.1 us
    sin x1, local copies, waits for them, and re-layouts, shards(): jnp.sin(angles)  8.15 us
    dot_general x12, matrix products, half(): jnp.einsum('rqk,kj->rqj', partner, lax.dynamic_index_in_dim(partner_map,...  4.77 us
    dot_general x6, matrix products, shards(): own = jnp.einsum('rqk,skj->srqj', kept_parts[i], own_map, precision=HIGH)  3.9 us
    dot_general x1, matrix products, shards(): outgoing = jnp.dot(placement, blocks, precision=HIGH)  3.86 us
  transfers between devices with their start and end apart: 7, of which 5 were waited for; matrix products, arithmetic and copies ran while one was open for 15% of the time, Pallas kernels for 0%

profile of v2, /device:TPU:256, one launch (start us, length us, event | category | flops | bytes accessed | tf_op | source)
XLA Modules:
  0.0 107.2 jit_solution(991776127025387974)
XLA Ops:
  0.0 0.0 copy-start
  0.8 1.0 fusion.5
  1.8 0.7 convert_add_fusion
  2.5 3.9 %fusion = f32[32,32,256]{2,1,0:T(8,128)} fusion(f32[512]{0:T(512)S(1)} %fusion.80, s32[512]{0:T(512)S(1)} %convert_add_fusion, s32[32,32]{1,0:T(8,128)S(1)} %multiply_add_fusion.12, f32[1,1,512,256]{3,2,1,0:T(8,128)} %param.7), kind=kOutput, calls=%fused_computation | convolution fusion | flops 1611661312 | bytes 1581056 | tf_op jit(solution)/shard_map/dot_general | solution.py:53
  6.3 0.0 copy-start.3
  6.3 13.1 %all-to-all-start = ((f32[32,32,256]{2,1,0:T(8,128)}), f32[32,32,256]{2,1,0:T(8,128)}, u32[]{:S(2)}, u32[]{:S(2)}) async-start(f32[32,32,256]{2,1,0:T(8,128)} %fusion), calls=%async_computation | async-start | bytes 2097152 | tf_op jit(solution)/shard_map/all_to_all | solution.py:54
  19.5 0.0 copy-done.3
  19.5 0.1 eq.53
  19.6 8.1 %sine_bitcast_fusion = (f32[3,512,256]{2,1,0:T(8,128)S(1)}, f32[3,512,256]{2,1,0:T(8,128)}) fusion(f32[1,1,3,512,256]{4,3,2,1,0:T(8,128)} %param.13), kind=kLoop, calls=%fused_computation.5 | loop fusion | bytes 4718592 | tf_op jit(solution)/shard_map/sin | solution.py:62
  27.7 0.0 copy-start.2
  27.7 21.2 %all-to-all-done = f32[32,32,256]{2,1,0:T(8,128)} async-done(((f32[32,32,256]{2,1,0:T(8,128)}), f32[32,32,256]{2,1,0:T(8,128)}, u32[]{:S(2)}, u32[]{:S(2)}) %all-to-all-start) | async-done | bytes 1048608 | tf_op jit(solution)/shard_map/all_to_all | solution.py:54
  48.9 2.5 %fusion.4 = f32[512,256,1]{1,0,2:T(8,128)S(1)} fusion(f32[1024,256]{1,0:T(8,128)} %bitcast.12, s32[1024]{0:T(1024)S(1)} %eq.53), kind=kOutput, calls=%fused_computation.7 | convolution fusion | flops 1611137024 | bytes 1576960 | tf_op jit(solution)/shard_map/dot_general | solution.py:63
  51.4 0.0 copy-done.2
  51.4 1.0 fusion.11
  52.6 0.0 copy-start.1
  52.6 0.0 copy-done
  52.6 0.6 fusion.17
  53.2 0.7 fusion.15
  53.9 7.6 %collective-permute-start = (f32[2,120,256]{2,1,0:T(8,128)S(1)}, f32[2,120,256]{2,1,0:T(8,128)S(1)}, u32[]{:S(2)}, u32[]{:S(2)}) collective-permute-start(f32[2,120,256]{2,1,0:T(8,128)S(1)} %dynamic-slice_bitcast_fusion.7), channel_id=1, source_target_pairs={{0,32},{32,0},{64,96},{96,64},{128,160},{160,128},{192,224},{224,1... | collective-permute-start | bytes 737288 | tf_op jit(solution)/shard_map/ppermute | solution.py:16
  61.5 1.9 %collective-permute-start.3 = (f32[2,136,256]{2,1,0:T(8,128)S(1)}, f32[2,136,256]{2,1,0:T(8,128)S(1)}, u32[]{:S(2)}, u32[]{:S(2)}) collective-permute-start(f32[2,136,256]{2,1,0:T(8,128)S(1)} %dynamic-slice_bitcast_fusion), channel_id=1, source_target_pairs={{0,32},{32,0},{64,96},{96,64},{128,160},{160,128},{192,224},{224,1... | collective-permute-start | bytes 835592 | tf_op jit(solution)/shard_map/ppermute | solution.py:16
  63.4 0.0 copy-done.1
  63.4 0.1 fusion.86
  63.6 4.5 %collective-permute-done = f32[2,120,256]{2,1,0:T(8,128)S(1)} collective-permute-done((f32[2,120,256]{2,1,0:T(8,128)S(1)}, f32[2,120,256]{2,1,0:T(8,128)S(1)}, u32[]{:S(2)}, u32[]{:S(2)}) %collective-permute-start) | collective-permute-done | bytes 245792 | tf_op jit(solution)/shard_map/ppermute | solution.py:16
  68.1 0.4 convolution_add_fusion.10
  68.5 0.4 convolution_add_fusion.11
  68.9 0.1 multiply_subtract_fusion.11
  69.0 1.9 %collective-permute-start.1 = (f32[2,120,256]{2,1,0:T(8,128)S(1)}, f32[2,120,256]{2,1,0:T(8,128)S(1)}, u32[]{:S(2)}, u32[]{:S(2)}) collective-permute-start(f32[2,120,256]{2,1,0:T(8,128)S(1)} %pad_maximum_fusion.2), channel_id=1, source_target_pairs={{0,64},{32,96},{64,0},{96,32},{128,192},{160,224},{192,128},{224,1... | collective-permute-start | bytes 737288 | tf_op jit(solution)/shard_map/ppermute | solution.py:16
  71.0 0.6 fusion.21
  71.6 2.2 %collective-permute-done.3 = f32[2,136,256]{2,1,0:T(8,128)S(1)} collective-permute-done((f32[2,136,256]{2,1,0:T(8,128)S(1)}, f32[2,136,256]{2,1,0:T(8,128)S(1)}, u32[]{:S(2)}, u32[]{:S(2)}) %collective-permute-start.3) | collective-permute-done | bytes 278560 | tf_op jit(solution)/shard_map/ppermute | solution.py:16
  73.8 0.4 convolution_add_fusion.4
  74.2 0.4 convolution_add_fusion.5
  74.6 0.1 multiply_subtract_fusion.5
  74.8 2.6 %collective-permute-start.4 = (f32[2,136,256]{2,1,0:T(8,128)S(1)}, f32[2,136,256]{2,1,0:T(8,128)S(1)}, u32[]{:S(2)}, u32[]{:S(2)}) collective-permute-start(f32[2,136,256]{2,1,0:T(8,128)S(1)} %pad_maximum_fusion), channel_id=1, source_target_pairs={{0,64},{32,96},{64,0},{96,32},{128,192},{160,224},{192,128},{224,1... | collective-permute-start | bytes 835592 | tf_op jit(solution)/shard_map/ppermute | solution.py:16
  77.4 0.7 fusion.19
  78.1 10.6 %collective-permute-done.1 = f32[2,120,256]{2,1,0:T(8,128)S(1)} collective-permute-done((f32[2,120,256]{2,1,0:T(8,128)S(1)}, f32[2,120,256]{2,1,0:T(8,128)S(1)}, u32[]{:S(2)}, u32[]{:S(2)}) %collective-permute-start.1) | collective-permute-done | bytes 245792 | tf_op jit(solution)/shard_map/ppermute | solution.py:16
  88.7 0.4 convolution_add_fusion.8
  89.1 0.4 convolution_add_fusion.9
  89.5 0.1 multiply_subtract_fusion.9
  89.7 5.4 %collective-permute-start.2 = (f32[2,120,256]{2,1,0:T(8,128)S(1)}, f32[2,120,256]{2,1,0:T(8,128)S(1)}, u32[]{:S(2)}, u32[]{:S(2)}) collective-permute-start(f32[2,120,256]{2,1,0:T(8,128)S(1)} %pad_maximum_fusion.3), channel_id=1, source_target_pairs={{0,128},{32,160},{64,192},{96,224},{128,0},{160,32},{192,64},{224,... | collective-permute-start | bytes 737288 | tf_op jit(solution)/shard_map/ppermute | solution.py:16
  95.0 0.6 fusion.25
  95.7 0.0 collective-permute-done.4
  95.7 0.4 convolution_add_fusion.2
  96.1 0.4 convolution_add_fusion.3
  96.5 0.1 multiply_subtract_fusion.3
  96.6 2.5 %collective-permute-start.5 = (f32[2,136,256]{2,1,0:T(8,128)S(1)}, f32[2,136,256]{2,1,0:T(8,128)S(1)}, u32[]{:S(2)}, u32[]{:S(2)}) collective-permute-start(f32[2,136,256]{2,1,0:T(8,128)S(1)} %pad_maximum_fusion.1), channel_id=1, source_target_pairs={{0,128},{32,160},{64,192},{96,224},{128,0},{160,32},{192,64},{224,... | collective-permute-start | bytes 835592 | tf_op jit(solution)/shard_map/ppermute | solution.py:16
  99.2 0.7 fusion.23
  99.9 0.0 collective-permute-done.2
  99.9 0.4 convolution_add_fusion.7
  100.2 0.4 convolution_add_fusion.6
  100.6 0.1 multiply_subtract_fusion.7
  100.8 4.3 %collective-permute-done.5 = f32[2,136,256]{2,1,0:T(8,128)S(1)} collective-permute-done((f32[2,136,256]{2,1,0:T(8,128)S(1)}, f32[2,136,256]{2,1,0:T(8,128)S(1)}, u32[]{:S(2)}, u32[]{:S(2)}) %collective-permute-start.5) | collective-permute-done | bytes 278560 | tf_op jit(solution)/shard_map/ppermute | solution.py:16
  105.1 0.4 convolution_add_fusion
  105.5 0.4 convolution_add_fusion.1
  105.9 0.1 multiply_subtract_fusion.1
  106.0 0.1 maximum_maximum_fusion
  106.1 1.0 copy.12
  (14 shorter events, 0.4 us)
Async XLA Ops:
  0.0 52.6 %copy-start = (f32[2,512,256]{2,1,0:T(8,128)S(1)}, f32[2,512,256]{2,1,0:T(8,128)}, u32[]{:S(2)}) copy-start(f32[2,512,256]{2,1,0:T(8,128)} %param.12) | copy-start | bytes 3145732
  6.3 13.2 %copy-start.3 = (s32[1,1,32,32]{3,2,1,0:T(8,128)S(1)}, s32[1,1,32,32]{3,2,1,0:T(8,128)}, u32[]{:S(2)}) copy-start(s32[1,1,32,32]{3,2,1,0:T(8,128)} %param.10) | copy-start | bytes 12292
  6.3 42.6 %all-to-all-start = ((f32[32,32,256]{2,1,0:T(8,128)}), f32[32,32,256]{2,1,0:T(8,128)}, u32[]{:S(2)}, u32[]{:S(2)}) async-start(f32[32,32,256]{2,1,0:T(8,128)} %fusion), calls=%async_computation | async-start | bytes 2097152 | tf_op jit(solution)/shard_map/all_to_all | solution.py:54
  27.7 23.7 %copy-start.2 = (f32[256,512]{1,0:T(8,128)S(1)}, f32[256,512]{1,0:T(8,128)}, u32[]{:S(2)}) copy-start(f32[256,512]{1,0:T(8,128)} %param.11) | copy-start | bytes 1572868
  52.6 10.9 %copy-start.1 = (f32[3,512,256]{2,1,0:T(8,128)S(1)}, f32[3,512,256]{2,1,0:T(8,128)}, u32[]{:S(2)}) copy-start(f32[3,512,256]{2,1,0:T(8,128)} %get-tuple-element.9) | copy-start | bytes 4718596
  53.9 14.2 %collective-permute-start = (f32[2,120,256]{2,1,0:T(8,128)S(1)}, f32[2,120,256]{2,1,0:T(8,128)S(1)}, u32[]{:S(2)}, u32[]{:S(2)}) collective-permute-start(f32[2,120,256]{2,1,0:T(8,128)S(1)} %dynamic-slice_bitcast_fusion.7), channel_id=1, source_target_pairs={{0,32},{32,0},{64,96},{96,64},{128,160},{160,128},{192,224},{224,1... | collective-permute-start | bytes 737288 | tf_op jit(solution)/shard_map/ppermute | solution.py:16
  61.5 12.3 %collective-permute-start.3 = (f32[2,136,256]{2,1,0:T(8,128)S(1)}, f32[2,136,256]{2,1,0:T(8,128)S(1)}, u32[]{:S(2)}, u32[]{:S(2)}) collective-permute-start(f32[2,136,256]{2,1,0:T(8,128)S(1)} %dynamic-slice_bitcast_fusion), channel_id=1, source_target_pairs={{0,32},{32,0},{64,96},{96,64},{128,160},{160,128},{192,224},{224,1... | collective-permute-start | bytes 835592 | tf_op jit(solution)/shard_map/ppermute | solution.py:16
  69.0 19.7 %collective-permute-start.1 = (f32[2,120,256]{2,1,0:T(8,128)S(1)}, f32[2,120,256]{2,1,0:T(8,128)S(1)}, u32[]{:S(2)}, u32[]{:S(2)}) collective-permute-start(f32[2,120,256]{2,1,0:T(8,128)S(1)} %pad_maximum_fusion.2), channel_id=1, source_target_pairs={{0,64},{32,96},{64,0},{96,32},{128,192},{160,224},{192,128},{224,1... | collective-permute-start | bytes 737288 | tf_op jit(solution)/shard_map/ppermute | solution.py:16
  74.8 20.9 %collective-permute-start.4 = (f32[2,136,256]{2,1,0:T(8,128)S(1)}, f32[2,136,256]{2,1,0:T(8,128)S(1)}, u32[]{:S(2)}, u32[]{:S(2)}) collective-permute-start(f32[2,136,256]{2,1,0:T(8,128)S(1)} %pad_maximum_fusion), channel_id=1, source_target_pairs={{0,64},{32,96},{64,0},{96,32},{128,192},{160,224},{192,128},{224,1... | collective-permute-start | bytes 835592 | tf_op jit(solution)/shard_map/ppermute | solution.py:16
  89.7 10.2 %collective-permute-start.2 = (f32[2,120,256]{2,1,0:T(8,128)S(1)}, f32[2,120,256]{2,1,0:T(8,128)S(1)}, u32[]{:S(2)}, u32[]{:S(2)}) collective-permute-start(f32[2,120,256]{2,1,0:T(8,128)S(1)} %pad_maximum_fusion.3), channel_id=1, source_target_pairs={{0,128},{32,160},{64,192},{96,224},{128,0},{160,32},{192,64},{224,... | collective-permute-start | bytes 737288 | tf_op jit(solution)/shard_map/ppermute | solution.py:16
  96.6 8.4 %collective-permute-start.5 = (f32[2,136,256]{2,1,0:T(8,128)S(1)}, f32[2,136,256]{2,1,0:T(8,128)S(1)}, u32[]{:S(2)}, u32[]{:S(2)}) collective-permute-start(f32[2,136,256]{2,1,0:T(8,128)S(1)} %pad_maximum_fusion.1), channel_id=1, source_target_pairs={{0,128},{32,160},{64,192},{96,224},{128,0},{160,32},{192,64},{224,... | collective-permute-start | bytes 835592 | tf_op jit(solution)/shard_map/ppermute | solution.py:16

commit v3 on v2

--- a/solution.py
+++ b/solution.py
@@ -60,22 +60,25 @@
     )
     angles = phase[0, 0]
     arrived, cosines, sines = lax.optimization_barrier((arrived, jnp.cos(angles), jnp.sin(angles)))
-    gathered = jnp.dot(selector, arrived.reshape(-1, trace_count), precision=HIGH)
-    weights_now = jnp.einsum(
-        "pt,trk->rpk", gathered, anterp.reshape(trace_count, 2, weight_count), precision=HIGH
-    )
     half_rows = pair_count // 2
     edges = [sum(CHUNK_ROWS[:i]) * half_rows // 256 for i in range(CHUNKS + 1)]
     cosines = cosines.reshape(LEVELS, 2, half_rows, weight_count)
     sines = sines.reshape(LEVELS, 2, half_rows, weight_count)
-    weights_now = weights_now.reshape(2, 2, half_rows, weight_count)
     box_index = lax.axis_index("box")
     bits = [box_index >> level_id & 1 for level_id in range(LEVELS)]
-    kept_parts, sent_parts = [], []
+    sources = arrived.reshape(-1, trace_count)
+    halves = selector.reshape(2, half_rows, -1)
+    anterp_parts = anterp.reshape(trace_count, 2, weight_count)
+
+    def initial(c, i):
+        chosen = lax.dynamic_index_in_dim(halves, c, 0, keepdims=False)[edges[i]:edges[i + 1]]
+        gathered = jnp.dot(chosen, sources, precision=HIGH)
+        return jnp.einsum("pt,trk->rpk", gathered, anterp_parts, precision=HIGH)
+
+    sent_parts, kept_parts = [], []
     for i in range(CHUNKS):
-        piece = weights_now[:, :, edges[i]:edges[i + 1]]
-        kept_parts.append(lax.dynamic_index_in_dim(piece, bits[0], 1, keepdims=False))
-        sent_parts.append(lax.dynamic_index_in_dim(piece, 1 - bits[0], 1, keepdims=False))
+        sent_parts.append(initial(1 - bits[0], i))
+        kept_parts.append(initial(bits[0], i))
     outputs = [None] * CHUNKS
     for level_id in range(LEVELS):
         side_bit = bits[level_id]

time: 108 us -> 107 us (level)
  the two profiles are of different devices: /device:TPU:256 before, /device:TPU:8 now
where the time goes in v3:
time: 107 us; the launch traced here: 106 us
  waiting for transfers between devices  43.5 us (41%)
  starting transfers between devices  32.3 us (30%)
  matrix products  17.4 us (16%)
  local copies, waits for them, and re-layouts  9.78 us (9%)
  other arithmetic  1.89 us (2%)
  between operations  1.17 us (1%)
    ppermute x6, waiting for transfers between devices, swapped(): lax.ppermute(x, axis, [(i, i ^ 1 << bit) for i in range(lax.axis_size(axi...  23.6 us
    all_to_all x1, waiting for transfers between devices, shards(): lax.all_to_all(outgoing.reshape(param_count, slot_count, trace_count), 'p...  19.9 us
    all_to_all x1, starting transfers between devices, shards(): lax.all_to_all(outgoing.reshape(param_count, slot_count, trace_count), 'p...  16.8 us
    ppermute x6, starting transfers between devices, swapped(): lax.ppermute(x, axis, [(i, i ^ 1 << bit) for i in range(lax.axis_size(axi...  15.5 us
    sin x1, local copies, waits for them, and re-layouts, shards(): jnp.sin(angles)  8.51 us
    dot_general x12, matrix products, half(): jnp.einsum('rqk,kj->rqj', partner, lax.dynamic_index_in_dim(partner_map,...  4.76 us
    dot_general x6, matrix products, shards(): own = jnp.einsum('rqk,skj->srqj', kept_parts[i], own_map, precision=HIGH)  3.9 us
    dot_general x1, matrix products, shards(): outgoing = jnp.dot(placement, blocks, precision=HIGH)  3.86 us
  transfers between devices with their start and end apart: 7, of which 7 were waited for; matrix products, arithmetic and copies ran while one was open for 17% of the time, Pallas kernels for 0%

profile of v3, /device:TPU:8, one launch (start us, length us, event | category | flops | bytes accessed | tf_op | source)
XLA Modules:
  0.0 106.0 jit_solution(17304127017060153921)
XLA Ops:
  0.0 0.0 copy-start
  0.8 1.0 fusion.3
  1.8 0.7 convert_add_fusion
  2.5 3.9 %fusion = f32[32,32,256]{2,1,0:T(8,128)} fusion(f32[512]{0:T(512)S(1)} %fusion.82, s32[512]{0:T(512)S(1)} %convert_add_fusion, s32[32,32]{1,0:T(8,128)S(1)} %multiply_add_fusion.12, f32[1,1,512,256]{3,2,1,0:T(8,128)} %param.7), kind=kOutput, calls=%fused_computation | convolution fusion | flops 1611661312 | bytes 1581056 | tf_op jit(solution)/shard_map/dot_general | solution.py:53
  6.3 16.8 %all-to-all-start = ((f32[32,32,256]{2,1,0:T(8,128)}), f32[32,32,256]{2,1,0:T(8,128)S(1)}, u32[]{:S(2)}, u32[]{:S(2)}) async-start(f32[32,32,256]{2,1,0:T(8,128)} %fusion), calls=%async_computation | async-start | bytes 2097152 | tf_op jit(solution)/shard_map/all_to_all | solution.py:54
  23.2 0.0 copy-done.4
  23.2 0.1 eq.63
  23.3 0.4 broadcast_compare_fusion
  23.6 8.5 %sine_bitcast_fusion = (f32[3,512,256]{2,1,0:T(8,128)}, f32[3,512,256]{2,1,0:T(8,128)}) fusion(f32[1,1,3,512,256]{4,3,2,1,0:T(8,128)} %param.13), kind=kLoop, calls=%fused_computation.3 | loop fusion | bytes 4718592 | tf_op jit(solution)/shard_map/sin | solution.py:62
  32.1 19.9 %all-to-all-done = f32[32,32,256]{2,1,0:T(8,128)S(1)} async-done(((f32[32,32,256]{2,1,0:T(8,128)}), f32[32,32,256]{2,1,0:T(8,128)S(1)}, u32[]{:S(2)}, u32[]{:S(2)}) %all-to-all-start) | async-done | bytes 1048608 | tf_op jit(solution)/shard_map/all_to_all | solution.py:54
  52.1 0.5 convolution_bitcast_fusion.6
  52.6 0.5 convolution_bitcast_fusion.7
  53.1 0.0 copy-start.1
  53.1 0.5 convolution_bitcast_fusion.5
  53.7 0.0 copy-start.3
  53.7 0.5 convolution_bitcast_fusion.4
  54.2 0.0 copy-start.2
  54.2 0.0 copy-done.1
  54.3 0.4 convolution_bitcast_fusion.2
  54.7 0.4 convolution_bitcast_fusion.3
  55.1 0.4 convolution_bitcast_fusion
  55.5 1.9 %collective-permute-start = (f32[2,120,256]{2,1,0:T(8,128)S(1)}, f32[2,120,256]{2,1,0:T(8,128)S(1)}, u32[]{:S(2)}, u32[]{:S(2)}) collective-permute-start(f32[2,120,256]{2,1,0:T(8,128)S(1)} %convolution_bitcast_fusion.2), channel_id=1, source_target_pairs={{0,32},{32,0},{64,96},{96,64},{128,160},{160,128},{192,224},{224,1... | collective-permute-start | bytes 737288 | tf_op jit(solution)/shard_map/ppermute | solution.py:16
  57.5 3.9 %collective-permute-start.3 = (f32[2,136,256]{2,1,0:T(8,128)S(1)}, f32[2,136,256]{2,1,0:T(8,128)S(1)}, u32[]{:S(2)}, u32[]{:S(2)}) collective-permute-start(f32[2,136,256]{2,1,0:T(8,128)S(1)} %convolution_bitcast_fusion), channel_id=1, source_target_pairs={{0,32},{32,0},{64,96},{96,64},{128,160},{160,128},{192,224},{224,1... | collective-permute-start | bytes 835592 | tf_op jit(solution)/shard_map/ppermute | solution.py:16
  61.4 0.0 copy-done.3
  61.4 0.0 copy-done.2
  61.4 0.1 fusion.88
  61.6 0.0 copy-done
  61.6 0.6 fusion.15
  62.2 0.4 convolution_bitcast_fusion.1
  62.7 0.7 fusion.13
  63.3 2.9 %collective-permute-done = f32[2,120,256]{2,1,0:T(8,128)S(1)} collective-permute-done((f32[2,120,256]{2,1,0:T(8,128)S(1)}, f32[2,120,256]{2,1,0:T(8,128)S(1)}, u32[]{:S(2)}, u32[]{:S(2)}) %collective-permute-start) | collective-permute-done | bytes 245792 | tf_op jit(solution)/shard_map/ppermute | solution.py:16
  66.3 0.4 convolution_add_fusion.10
  66.7 0.4 convolution_add_fusion.11
  67.1 0.1 multiply_subtract_fusion.11
  67.2 1.9 %collective-permute-start.1 = (f32[2,120,256]{2,1,0:T(8,128)S(1)}, f32[2,120,256]{2,1,0:T(8,128)S(1)}, u32[]{:S(2)}, u32[]{:S(2)}) collective-permute-start(f32[2,120,256]{2,1,0:T(8,128)S(1)} %pad_maximum_fusion.2), channel_id=1, source_target_pairs={{0,64},{32,96},{64,0},{96,32},{128,192},{160,224},{192,128},{224,1... | collective-permute-start | bytes 737288 | tf_op jit(solution)/shard_map/ppermute | solution.py:16
  69.1 0.6 fusion.19
  69.8 1.3 %collective-permute-done.3 = f32[2,136,256]{2,1,0:T(8,128)S(1)} collective-permute-done((f32[2,136,256]{2,1,0:T(8,128)S(1)}, f32[2,136,256]{2,1,0:T(8,128)S(1)}, u32[]{:S(2)}, u32[]{:S(2)}) %collective-permute-start.3) | collective-permute-done | bytes 278560 | tf_op jit(solution)/shard_map/ppermute | solution.py:16
  71.1 0.4 convolution_add_fusion.4
  71.5 0.4 convolution_add_fusion.5
  71.9 0.1 multiply_subtract_fusion.5
  72.0 3.7 %collective-permute-start.4 = (f32[2,136,256]{2,1,0:T(8,128)S(1)}, f32[2,136,256]{2,1,0:T(8,128)S(1)}, u32[]{:S(2)}, u32[]{:S(2)}) collective-permute-start(f32[2,136,256]{2,1,0:T(8,128)S(1)} %pad_maximum_fusion), channel_id=1, source_target_pairs={{0,64},{32,96},{64,0},{96,32},{128,192},{160,224},{192,128},{224,1... | collective-permute-start | bytes 835592 | tf_op jit(solution)/shard_map/ppermute | solution.py:16
  75.8 0.7 fusion.17
  76.4 10.4 %collective-permute-done.1 = f32[2,120,256]{2,1,0:T(8,128)S(1)} collective-permute-done((f32[2,120,256]{2,1,0:T(8,128)S(1)}, f32[2,120,256]{2,1,0:T(8,128)S(1)}, u32[]{:S(2)}, u32[]{:S(2)}) %collective-permute-start.1) | collective-permute-done | bytes 245792 | tf_op jit(solution)/shard_map/ppermute | solution.py:16
  86.9 0.4 convolution_add_fusion.8
  87.3 0.4 convolution_add_fusion.9
  87.7 0.1 multiply_subtract_fusion.9
  87.8 2.1 %collective-permute-start.2 = (f32[2,120,256]{2,1,0:T(8,128)S(1)}, f32[2,120,256]{2,1,0:T(8,128)S(1)}, u32[]{:S(2)}, u32[]{:S(2)}) collective-permute-start(f32[2,120,256]{2,1,0:T(8,128)S(1)} %pad_maximum_fusion.3), channel_id=1, source_target_pairs={{0,128},{32,160},{64,192},{96,224},{128,0},{160,32},{192,64},{224,... | collective-permute-start | bytes 737288 | tf_op jit(solution)/shard_map/ppermute | solution.py:16
  89.9 0.6 fusion.23
  90.5 2.1 %collective-permute-done.4 = f32[2,136,256]{2,1,0:T(8,128)S(1)} collective-permute-done((f32[2,136,256]{2,1,0:T(8,128)S(1)}, f32[2,136,256]{2,1,0:T(8,128)S(1)}, u32[]{:S(2)}, u32[]{:S(2)}) %collective-permute-start.4) | collective-permute-done | bytes 278560 | tf_op jit(solution)/shard_map/ppermute | solution.py:16
  92.6 0.4 convolution_add_fusion.2
  93.0 0.4 convolution_add_fusion.3
  93.4 0.1 multiply_subtract_fusion.3
  93.5 1.9 %collective-permute-start.5 = (f32[2,136,256]{2,1,0:T(8,128)S(1)}, f32[2,136,256]{2,1,0:T(8,128)S(1)}, u32[]{:S(2)}, u32[]{:S(2)}) collective-permute-start(f32[2,136,256]{2,1,0:T(8,128)S(1)} %pad_maximum_fusion.1), channel_id=1, source_target_pairs={{0,128},{32,160},{64,192},{96,224},{128,0},{160,32},{192,64},{224,... | collective-permute-start | bytes 835592 | tf_op jit(solution)/shard_map/ppermute | solution.py:16
  95.5 0.7 fusion.21
  96.2 1.0 collective-permute-done.2
  97.2 0.4 convolution_add_fusion.7
  97.6 0.4 convolution_add_fusion.6
  97.9 0.1 multiply_subtract_fusion.7
  98.1 5.8 %collective-permute-done.5 = f32[2,136,256]{2,1,0:T(8,128)S(1)} collective-permute-done((f32[2,136,256]{2,1,0:T(8,128)S(1)}, f32[2,136,256]{2,1,0:T(8,128)S(1)}, u32[]{:S(2)}, u32[]{:S(2)}) %collective-permute-start.5) | collective-permute-done | bytes 278560 | tf_op jit(solution)/shard_map/ppermute | solution.py:16
  103.9 0.4 convolution_add_fusion
  104.3 0.4 convolution_add_fusion.1
  104.7 0.1 multiply_subtract_fusion.1
  104.8 0.1 maximum_maximum_fusion
  104.9 1.0 copy.17
  (12 shorter events, 0.2 us)
Async XLA Ops:
  0.0 61.6 %copy-start = (f32[2,512,256]{2,1,0:T(8,128)S(1)}, f32[2,512,256]{2,1,0:T(8,128)}, u32[]{:S(2)}) copy-start(f32[2,512,256]{2,1,0:T(8,128)} %param.12) | copy-start | bytes 3145732
  6.3 16.8 %copy-start.4 = (s32[1,1,32,32]{3,2,1,0:T(8,128)S(1)}, s32[1,1,32,32]{3,2,1,0:T(8,128)}, u32[]{:S(2)}) copy-start(s32[1,1,32,32]{3,2,1,0:T(8,128)} %param.10) | copy-start | bytes 12292
  6.3 45.7 %all-to-all-start = ((f32[32,32,256]{2,1,0:T(8,128)}), f32[32,32,256]{2,1,0:T(8,128)S(1)}, u32[]{:S(2)}, u32[]{:S(2)}) async-start(f32[32,32,256]{2,1,0:T(8,128)} %fusion), calls=%async_computation | async-start | bytes 2097152 | tf_op jit(solution)/shard_map/all_to_all | solution.py:54
  53.1 1.1 %copy-start.1 = (f32[256,512]{1,0:T(8,128)S(1)}, f32[256,512]{1,0:T(8,128)}, u32[]{:S(2)}) copy-start(f32[256,512]{1,0:T(8,128)} %param.11) | copy-start | bytes 1572868
  53.7 7.7 %copy-start.3 = (f32[3,512,256]{2,1,0:T(8,128)S(1)}, f32[3,512,256]{2,1,0:T(8,128)}, u32[]{:S(2)}) copy-start(f32[3,512,256]{2,1,0:T(8,128)} %get-tuple-element.9) | copy-start | bytes 4718596
  54.2 7.2 %copy-start.2 = (f32[3,512,256]{2,1,0:T(8,128)S(1)}, f32[3,512,256]{2,1,0:T(8,128)}, u32[]{:S(2)}) copy-start(f32[3,512,256]{2,1,0:T(8,128)} %get-tuple-element.10) | copy-start | bytes 4718596
  55.5 10.7 %collective-permute-start = (f32[2,120,256]{2,1,0:T(8,128)S(1)}, f32[2,120,256]{2,1,0:T(8,128)S(1)}, u32[]{:S(2)}, u32[]{:S(2)}) collective-permute-start(f32[2,120,256]{2,1,0:T(8,128)S(1)} %convolution_bitcast_fusion.2), channel_id=1, source_target_pairs={{0,32},{32,0},{64,96},{96,64},{128,160},{160,128},{192,224},{224,1... | collective-permute-start | bytes 737288 | tf_op jit(solution)/shard_map/ppermute | solution.py:16
  57.5 13.6 %collective-permute-start.3 = (f32[2,136,256]{2,1,0:T(8,128)S(1)}, f32[2,136,256]{2,1,0:T(8,128)S(1)}, u32[]{:S(2)}, u32[]{:S(2)}) collective-permute-start(f32[2,136,256]{2,1,0:T(8,128)S(1)} %convolution_bitcast_fusion), channel_id=1, source_target_pairs={{0,32},{32,0},{64,96},{96,64},{128,160},{160,128},{192,224},{224,1... | collective-permute-start | bytes 835592 | tf_op jit(solution)/shard_map/ppermute | solution.py:16
  67.2 19.7 %collective-permute-start.1 = (f32[2,120,256]{2,1,0:T(8,128)S(1)}, f32[2,120,256]{2,1,0:T(8,128)S(1)}, u32[]{:S(2)}, u32[]{:S(2)}) collective-permute-start(f32[2,120,256]{2,1,0:T(8,128)S(1)} %pad_maximum_fusion.2), channel_id=1, source_target_pairs={{0,64},{32,96},{64,0},{96,32},{128,192},{160,224},{192,128},{224,1... | collective-permute-start | bytes 737288 | tf_op jit(solution)/shard_map/ppermute | solution.py:16
  72.0 20.6 %collective-permute-start.4 = (f32[2,136,256]{2,1,0:T(8,128)S(1)}, f32[2,136,256]{2,1,0:T(8,128)S(1)}, u32[]{:S(2)}, u32[]{:S(2)}) collective-permute-start(f32[2,136,256]{2,1,0:T(8,128)S(1)} %pad_maximum_fusion), channel_id=1, source_target_pairs={{0,64},{32,96},{64,0},{96,32},{128,192},{160,224},{192,128},{224,1... | collective-permute-start | bytes 835592 | tf_op jit(solution)/shard_map/ppermute | solution.py:16
  87.8 9.4 %collective-permute-start.2 = (f32[2,120,256]{2,1,0:T(8,128)S(1)}, f32[2,120,256]{2,1,0:T(8,128)S(1)}, u32[]{:S(2)}, u32[]{:S(2)}) collective-permute-start(f32[2,120,256]{2,1,0:T(8,128)S(1)} %pad_maximum_fusion.3), channel_id=1, source_target_pairs={{0,128},{32,160},{64,192},{96,224},{128,0},{160,32},{192,64},{224,... | collective-permute-start | bytes 737288 | tf_op jit(solution)/shard_map/ppermute | solution.py:16
  93.5 10.3 %collective-permute-start.5 = (f32[2,136,256]{2,1,0:T(8,128)S(1)}, f32[2,136,256]{2,1,0:T(8,128)S(1)}, u32[]{:S(2)}, u32[]{:S(2)}) collective-permute-start(f32[2,136,256]{2,1,0:T(8,128)S(1)} %pad_maximum_fusion.1), channel_id=1, source_target_pairs={{0,128},{32,160},{64,192},{96,224},{128,0},{160,32},{192,64},{224,... | collective-permute-start | bytes 835592 | tf_op jit(solution)/shard_map/ppermute | solution.py:16

commit v4 on v3

--- a/solution.py
+++ b/solution.py
@@ -50,7 +50,12 @@
     )
     slots = jnp.arange(param_count * slot_count, dtype=jnp.int32)
     placement = jnp.where(slots[:, None] == position[None, :], live_mask[None, :], 0.0)
-    outgoing = jnp.dot(placement, blocks, precision=HIGH)
+    top = lax.reduce_precision(blocks, exponent_bits=8, mantissa_bits=7)
+    rest = blocks - top
+    middle = lax.reduce_precision(rest, exponent_bits=8, mantissa_bits=7)
+    pieces = jnp.concatenate([top, middle, rest - middle], axis=0).astype(jnp.bfloat16)
+    stacked = jnp.concatenate([placement] * 3, axis=1).astype(jnp.bfloat16)
+    outgoing = jnp.dot(stacked, pieces, preferred_element_type=jnp.float32)
     arrived = lax.all_to_all(
         outgoing.reshape(param_count, slot_count, trace_count),
         "param",
@@ -79,7 +84,7 @@
     for i in range(CHUNKS):
         sent_parts.append(initial(1 - bits[0], i))
         kept_parts.append(initial(bits[0], i))
-    outputs = [None] * CHUNKS
+    result = jnp.zeros((2, pair_count, weight_count), jnp.float32)
     for level_id in range(LEVELS):
         side_bit = bits[level_id]
         own_map = lax.dynamic_slice_in_dim(interp, side_bit * half_rows, half_rows, 1)
@@ -105,9 +110,9 @@
                 sent_parts[i] = half(1 - next_bit)
                 kept_parts[i] = half(next_bit)
             else:
-                outputs[i] = jnp.stack([half(0), half(1)], axis=1)
-    weights_now = jnp.concatenate(outputs, axis=2).reshape(2, pair_count, weight_count)
-    return weights_now[None, None]
+                for s in range(2):
+                    result = result.at[:, s * half_rows + edges[i]:s * half_rows + edges[i + 1]].set(half(s))
+    return result[None, None]
 
 
 def solution(mesh):

time: 107 us -> 107 us (level)
  other arithmetic: 1.89 us -> 4.04 us
  matrix products: 17.4 us -> 15.5 us
    dot_general x1, matrix products: 3.86 us -> 1.95 us  [shards(): outgoing = jnp.dot(stacked, pieces, preferred_element_type=jnp.float32)]
    another operation x4 -> x2, other arithmetic: 0.11 us -> 1.51 us  [shards(): outputs[i] = jnp.stack([half(0), half(1)], axis=1)]
where the time goes in v4:
time: 107 us; the launch traced here: 106 us
  waiting for transfers between devices  43.3 us (40%)
  starting transfers between devices  32.3 us (30%)
  matrix products  15.5 us (14%)
  local copies, waits for them, and re-layouts  9.69 us (9%)
  other arithmetic  4.04 us (4%)
  between operations  1.2 us (1%)
    ppermute x6, waiting for transfers between devices, swapped(): lax.ppermute(x, axis, [(i, i ^ 1 << bit) for i in range(lax.axis_size(axi...  23.4 us
    all_to_all x1, waiting for transfers between devices, shards(): lax.all_to_all(outgoing.reshape(param_count, slot_count, trace_count), 'p...  20 us
    all_to_all x1, starting transfers between devices, shards(): lax.all_to_all(outgoing.reshape(param_count, slot_count, trace_count), 'p...  16.8 us
    ppermute x6, starting transfers between devices, swapped(): lax.ppermute(x, axis, [(i, i ^ 1 << bit) for i in range(lax.axis_size(axi...  15.5 us
    sin x1, local copies, waits for them, and re-layouts, shards(): jnp.sin(angles)  8.49 us
    dot_general x12, matrix products, half(): jnp.einsum('rqk,kj->rqj', partner, lax.dynamic_index_in_dim(partner_map,...  4.76 us
    dot_general x6, matrix products, shards(): own = jnp.einsum('rqk,skj->srqj', kept_parts[i], own_map, precision=HIGH)  3.91 us
  transfers between devices with their start and end apart: 7, of which 7 were waited for; matrix products, arithmetic and copies ran while one was open for 17% of the time, Pallas kernels for 0%

profile of v4, /device:TPU:8, one launch (start us, length us, event | category | flops | bytes accessed | tf_op | source)
XLA Modules:
  0.0 106.0 jit_solution(16084818905690983950)
XLA Ops:
  0.0 0.0 copy-start
  0.8 1.0 fusion.6
  1.8 0.7 convert_add_fusion
  2.5 1.2 %reduce-precision_convert_fusion.1 = (bf16[512,256]{1,0:T(8,128)(2,1)S(1)}, bf16[512,256]{1,0:T(8,128)(2,1)S(1)}, bf16[512,256]{1,0:T(8,128)(2,1)S(1)}) fusion(f32[1,1,512,256]{3,2,1,0:T(8,128)} %param.15), kind=kLoop, calls=%fused_computation.45 | loop fusion | flops 917504 | bytes 1310720 | tf_op jit(solution)/shard_map/convert
  3.6 0.3 select_convert_fusion
  4.0 1.9 %fusion = f32[1024,256]{1,0:T(8,128)} fusion(bf16[1024,512]{1,0:T(8,128)(2,1)S(1)} %select_convert_fusion, bf16[512,256]{1,0:T(8,128)(2,1)S(1)} %get-tuple-element.102, bf16[512,256]{1,0:T(8,128)(2,1)S(1)} %get-tuple-element.103, bf16[512,256]{1,0:T(8,128)(2,1)S(1)} %get-tuple-element.101), kind=kOutput, calls=%fused_computation | convolution fusion | flops 817102848 | bytes 2883584 | tf_op jit(solution)/shard_map/dot_general | solution.py:58
  5.9 16.8 %all-to-all-start = ((f32[32,32,256]{2,1,0:T(8,128)}), f32[32,32,256]{2,1,0:T(8,128)S(1)}, u32[]{:S(2)}, u32[]{:S(2)}) async-start(f32[32,32,256]{2,1,0:T(8,128)} %bitcast.10), calls=%async_computation | async-start | bytes 2097152 | tf_op jit(solution)/shard_map/all_to_all | solution.py:59
  22.8 0.0 copy-done.5
  22.8 0.1 eq.52
  22.9 0.4 broadcast_compare_fusion
  23.2 8.5 %sine_bitcast_fusion = (f32[3,512,256]{2,1,0:T(8,128)}, f32[3,512,256]{2,1,0:T(8,128)}) fusion(f32[1,1,3,512,256]{4,3,2,1,0:T(8,128)} %param.21), kind=kLoop, calls=%fused_computation.8 | loop fusion | bytes 4718592 | tf_op jit(solution)/shard_map/sin | solution.py:67
  31.7 20.0 %all-to-all-done = f32[32,32,256]{2,1,0:T(8,128)S(1)} async-done(((f32[32,32,256]{2,1,0:T(8,128)}), f32[32,32,256]{2,1,0:T(8,128)S(1)}, u32[]{:S(2)}, u32[]{:S(2)}) %all-to-all-start) | async-done | bytes 1048608 | tf_op jit(solution)/shard_map/all_to_all | solution.py:59
  51.7 0.5 convolution_bitcast_fusion.6
  52.2 0.5 convolution_bitcast_fusion.7
  52.7 0.0 copy-start.1
  52.8 0.5 convolution_bitcast_fusion.5
  53.3 0.0 copy-start.3
  53.3 0.5 convolution_bitcast_fusion.4
  53.9 0.0 copy-start.2
  53.9 0.4 convolution_bitcast_fusion.2
  54.3 0.4 convolution_bitcast_fusion.3
  54.7 0.4 convolution_bitcast_fusion
  55.2 1.9 %collective-permute-start = (f32[2,120,256]{2,1,0:T(8,128)S(1)}, f32[2,120,256]{2,1,0:T(8,128)S(1)}, u32[]{:S(2)}, u32[]{:S(2)}) collective-permute-start(f32[2,120,256]{2,1,0:T(8,128)S(1)} %convolution_bitcast_fusion.2), channel_id=1, source_target_pairs={{0,32},{32,0},{64,96},{96,64},{128,160},{160,128},{192,224},{224,1... | collective-permute-start | bytes 737288 | tf_op jit(solution)/shard_map/ppermute | solution.py:16
  57.1 3.9 %collective-permute-start.3 = (f32[2,136,256]{2,1,0:T(8,128)S(1)}, f32[2,136,256]{2,1,0:T(8,128)S(1)}, u32[]{:S(2)}, u32[]{:S(2)}) collective-permute-start(f32[2,136,256]{2,1,0:T(8,128)S(1)} %convolution_bitcast_fusion), channel_id=1, source_target_pairs={{0,32},{32,0},{64,96},{96,64},{128,160},{160,128},{192,224},{224,1... | collective-permute-start | bytes 835592 | tf_op jit(solution)/shard_map/ppermute | solution.py:16
  61.1 0.1 fusion.96
  61.2 0.6 fusion.20
  61.8 0.4 convolution_bitcast_fusion.1
  62.3 0.7 fusion.18
  63.0 2.9 %collective-permute-done = f32[2,120,256]{2,1,0:T(8,128)S(1)} collective-permute-done((f32[2,120,256]{2,1,0:T(8,128)S(1)}, f32[2,120,256]{2,1,0:T(8,128)S(1)}, u32[]{:S(2)}, u32[]{:S(2)}) %collective-permute-start) | collective-permute-done | bytes 245792 | tf_op jit(solution)/shard_map/ppermute | solution.py:16
  65.9 0.4 convolution_add_fusion.10
  66.3 0.4 convolution_add_fusion.11
  66.7 0.1 multiply_subtract_fusion.11
  66.8 1.9 %collective-permute-start.1 = (f32[2,120,256]{2,1,0:T(8,128)S(1)}, f32[2,120,256]{2,1,0:T(8,128)S(1)}, u32[]{:S(2)}, u32[]{:S(2)}) collective-permute-start(f32[2,120,256]{2,1,0:T(8,128)S(1)} %pad_maximum_fusion.2), channel_id=1, source_target_pairs={{0,64},{32,96},{64,0},{96,32},{128,192},{160,224},{192,128},{224,1... | collective-permute-start | bytes 737288 | tf_op jit(solution)/shard_map/ppermute | solution.py:16
  68.8 0.6 fusion.24
  69.4 1.3 %collective-permute-done.3 = f32[2,136,256]{2,1,0:T(8,128)S(1)} collective-permute-done((f32[2,136,256]{2,1,0:T(8,128)S(1)}, f32[2,136,256]{2,1,0:T(8,128)S(1)}, u32[]{:S(2)}, u32[]{:S(2)}) %collective-permute-start.3) | collective-permute-done | bytes 278560 | tf_op jit(solution)/shard_map/ppermute | solution.py:16
  70.7 0.4 convolution_add_fusion.4
  71.1 0.4 convolution_add_fusion.5
  71.5 0.1 multiply_subtract_fusion.5
  71.6 3.7 %collective-permute-start.4 = (f32[2,136,256]{2,1,0:T(8,128)S(1)}, f32[2,136,256]{2,1,0:T(8,128)S(1)}, u32[]{:S(2)}, u32[]{:S(2)}) collective-permute-start(f32[2,136,256]{2,1,0:T(8,128)S(1)} %pad_maximum_fusion), channel_id=1, source_target_pairs={{0,64},{32,96},{64,0},{96,32},{128,192},{160,224},{192,128},{224,1... | collective-permute-start | bytes 835592 | tf_op jit(solution)/shard_map/ppermute | solution.py:16
  75.4 0.7 fusion.22
  76.1 10.4 %collective-permute-done.1 = f32[2,120,256]{2,1,0:T(8,128)S(1)} collective-permute-done((f32[2,120,256]{2,1,0:T(8,128)S(1)}, f32[2,120,256]{2,1,0:T(8,128)S(1)}, u32[]{:S(2)}, u32[]{:S(2)}) %collective-permute-start.1) | collective-permute-done | bytes 245792 | tf_op jit(solution)/shard_map/ppermute | solution.py:16
  86.5 0.4 convolution_add_fusion.8
  86.9 0.4 convolution_add_fusion.9
  87.3 0.1 multiply_subtract_fusion.9
  87.4 2.1 %collective-permute-start.2 = (f32[2,120,256]{2,1,0:T(8,128)S(1)}, f32[2,120,256]{2,1,0:T(8,128)S(1)}, u32[]{:S(2)}, u32[]{:S(2)}) collective-permute-start(f32[2,120,256]{2,1,0:T(8,128)S(1)} %pad_maximum_fusion.3), channel_id=1, source_target_pairs={{0,128},{32,160},{64,192},{96,224},{128,0},{160,32},{192,64},{224,... | collective-permute-start | bytes 737288 | tf_op jit(solution)/shard_map/ppermute | solution.py:16
  89.5 0.6 fusion.28
  90.1 2.0 %collective-permute-done.4 = f32[2,136,256]{2,1,0:T(8,128)S(1)} collective-permute-done((f32[2,136,256]{2,1,0:T(8,128)S(1)}, f32[2,136,256]{2,1,0:T(8,128)S(1)}, u32[]{:S(2)}, u32[]{:S(2)}) %collective-permute-start.4) | collective-permute-done | bytes 278560 | tf_op jit(solution)/shard_map/ppermute | solution.py:16
  92.2 0.4 convolution_add_fusion.2
  92.6 0.4 convolution_add_fusion.3
  93.0 0.1 multiply_subtract_fusion.3
  93.1 1.9 %collective-permute-start.5 = (f32[2,136,256]{2,1,0:T(8,128)S(1)}, f32[2,136,256]{2,1,0:T(8,128)S(1)}, u32[]{:S(2)}, u32[]{:S(2)}) collective-permute-start(f32[2,136,256]{2,1,0:T(8,128)S(1)} %pad_maximum_fusion.1), channel_id=1, source_target_pairs={{0,128},{32,160},{64,192},{96,224},{128,0},{160,32},{192,64},{224,... | collective-permute-start | bytes 835592 | tf_op jit(solution)/shard_map/ppermute | solution.py:16
  95.0 0.7 fusion.26
  95.7 1.0 collective-permute-done.2
  96.7 0.4 convolution_add_fusion.7
  97.1 0.4 convolution_add_fusion.6
  97.4 0.1 multiply_subtract_fusion.6
  97.5 0.1 fusion.7
  97.6 5.7 %collective-permute-done.5 = f32[2,136,256]{2,1,0:T(8,128)S(1)} collective-permute-done((f32[2,136,256]{2,1,0:T(8,128)S(1)}, f32[2,136,256]{2,1,0:T(8,128)S(1)}, u32[]{:S(2)}, u32[]{:S(2)}) %collective-permute-start.5) | collective-permute-done | bytes 278560 | tf_op jit(solution)/shard_map/ppermute | solution.py:16
  103.4 0.4 convolution_add_fusion
  103.8 0.4 convolution_add_fusion.1
  104.2 0.1 multiply_subtract_fusion
  104.3 0.0 copy-start.4
  104.3 1.0 copy-done.4
  105.3 0.7 fusion.45
  (13 shorter events, 0.2 us)
Async XLA Ops:
  0.0 61.2 %copy-start = (f32[2,512,256]{2,1,0:T(8,128)S(1)}, f32[2,512,256]{2,1,0:T(8,128)}, u32[]{:S(2)}) copy-start(f32[2,512,256]{2,1,0:T(8,128)} %param.20) | copy-start | bytes 3145732
  5.9 16.8 %copy-start.5 = (s32[1,1,32,32]{3,2,1,0:T(8,128)S(1)}, s32[1,1,32,32]{3,2,1,0:T(8,128)}, u32[]{:S(2)}) copy-start(s32[1,1,32,32]{3,2,1,0:T(8,128)} %param.18) | copy-start | bytes 12292
  5.9 45.7 %all-to-all-start = ((f32[32,32,256]{2,1,0:T(8,128)}), f32[32,32,256]{2,1,0:T(8,128)S(1)}, u32[]{:S(2)}, u32[]{:S(2)}) async-start(f32[32,32,256]{2,1,0:T(8,128)} %bitcast.10), calls=%async_computation | async-start | bytes 2097152 | tf_op jit(solution)/shard_map/all_to_all | solution.py:59
  52.7 1.1 %copy-start.1 = (f32[256,512]{1,0:T(8,128)S(1)}, f32[256,512]{1,0:T(8,128)}, u32[]{:S(2)}) copy-start(f32[256,512]{1,0:T(8,128)} %param.19) | copy-start | bytes 1572868
  53.3 7.7 %copy-start.3 = (f32[3,512,256]{2,1,0:T(8,128)S(1)}, f32[3,512,256]{2,1,0:T(8,128)}, u32[]{:S(2)}) copy-start(f32[3,512,256]{2,1,0:T(8,128)} %get-tuple-element.57) | copy-start | bytes 4718596
  53.9 7.2 %copy-start.2 = (f32[3,512,256]{2,1,0:T(8,128)S(1)}, f32[3,512,256]{2,1,0:T(8,128)}, u32[]{:S(2)}) copy-start(f32[3,512,256]{2,1,0:T(8,128)} %get-tuple-element.58) | copy-start | bytes 4718596
  55.2 10.7 %collective-permute-start = (f32[2,120,256]{2,1,0:T(8,128)S(1)}, f32[2,120,256]{2,1,0:T(8,128)S(1)}, u32[]{:S(2)}, u32[]{:S(2)}) collective-permute-start(f32[2,120,256]{2,1,0:T(8,128)S(1)} %convolution_bitcast_fusion.2), channel_id=1, source_target_pairs={{0,32},{32,0},{64,96},{96,64},{128,160},{160,128},{192,224},{224,1... | collective-permute-start | bytes 737288 | tf_op jit(solution)/shard_map/ppermute | solution.py:16
  57.1 13.6 %collective-permute-start.3 = (f32[2,136,256]{2,1,0:T(8,128)S(1)}, f32[2,136,256]{2,1,0:T(8,128)S(1)}, u32[]{:S(2)}, u32[]{:S(2)}) collective-permute-start(f32[2,136,256]{2,1,0:T(8,128)S(1)} %convolution_bitcast_fusion), channel_id=1, source_target_pairs={{0,32},{32,0},{64,96},{96,64},{128,160},{160,128},{192,224},{224,1... | collective-permute-start | bytes 835592 | tf_op jit(solution)/shard_map/ppermute | solution.py:16
  66.8 19.7 %collective-permute-start.1 = (f32[2,120,256]{2,1,0:T(8,128)S(1)}, f32[2,120,256]{2,1,0:T(8,128)S(1)}, u32[]{:S(2)}, u32[]{:S(2)}) collective-permute-start(f32[2,120,256]{2,1,0:T(8,128)S(1)} %pad_maximum_fusion.2), channel_id=1, source_target_pairs={{0,64},{32,96},{64,0},{96,32},{128,192},{160,224},{192,128},{224,1... | collective-permute-start | bytes 737288 | tf_op jit(solution)/shard_map/ppermute | solution.py:16
  71.6 20.5 %collective-permute-start.4 = (f32[2,136,256]{2,1,0:T(8,128)S(1)}, f32[2,136,256]{2,1,0:T(8,128)S(1)}, u32[]{:S(2)}, u32[]{:S(2)}) collective-permute-start(f32[2,136,256]{2,1,0:T(8,128)S(1)} %pad_maximum_fusion), channel_id=1, source_target_pairs={{0,64},{32,96},{64,0},{96,32},{128,192},{160,224},{192,128},{224,1... | collective-permute-start | bytes 835592 | tf_op jit(solution)/shard_map/ppermute | solution.py:16
  87.4 9.3 %collective-permute-start.2 = (f32[2,120,256]{2,1,0:T(8,128)S(1)}, f32[2,120,256]{2,1,0:T(8,128)S(1)}, u32[]{:S(2)}, u32[]{:S(2)}) collective-permute-start(f32[2,120,256]{2,1,0:T(8,128)S(1)} %pad_maximum_fusion.3), channel_id=1, source_target_pairs={{0,128},{32,160},{64,192},{96,224},{128,0},{160,32},{192,64},{224,... | collective-permute-start | bytes 737288 | tf_op jit(solution)/shard_map/ppermute | solution.py:16
  93.1 10.3 %collective-permute-start.5 = (f32[2,136,256]{2,1,0:T(8,128)S(1)}, f32[2,136,256]{2,1,0:T(8,128)S(1)}, u32[]{:S(2)}, u32[]{:S(2)}) collective-permute-start(f32[2,136,256]{2,1,0:T(8,128)S(1)} %pad_maximum_fusion.1), channel_id=1, source_target_pairs={{0,128},{32,160},{64,192},{96,224},{128,0},{160,32},{192,64},{224,... | collective-permute-start | bytes 835592 | tf_op jit(solution)/shard_map/ppermute | solution.py:16
  104.3 1.0 copy-start.4

commit v5 on v3

--- a/solution.py
+++ b/solution.py
@@ -5,7 +5,7 @@
 
 
 LEVELS = 3
-CHUNK_ROWS = (120, 136)
+CHUNK_ROWS = (144, 112)
 CHUNKS = len(CHUNK_ROWS)
 
 
@@ -50,7 +50,12 @@
     )
     slots = jnp.arange(param_count * slot_count, dtype=jnp.int32)
     placement = jnp.where(slots[:, None] == position[None, :], live_mask[None, :], 0.0)
-    outgoing = jnp.dot(placement, blocks, precision=HIGH)
+    top = lax.reduce_precision(blocks, exponent_bits=8, mantissa_bits=7)
+    rest = blocks - top
+    middle = lax.reduce_precision(rest, exponent_bits=8, mantissa_bits=7)
+    pieces = jnp.concatenate([top, middle, rest - middle], axis=0).astype(jnp.bfloat16)
+    stacked = jnp.concatenate([placement] * 3, axis=1).astype(jnp.bfloat16)
+    outgoing = jnp.dot(stacked, pieces, preferred_element_type=jnp.float32)
     arrived = lax.all_to_all(
         outgoing.reshape(param_count, slot_count, trace_count),
         "param",

time: 107 us -> 107 us (level)
  the two profiles are of different devices: /device:TPU:8 before, /device:TPU:256 now
where the time goes in v5:
time: 107 us; the launch traced here: 106 us
  waiting for transfers between devices  40.2 us (38%)
  starting transfers between devices  35.8 us (33%)
  matrix products  15.5 us (14%)
  local copies, waits for them, and re-layouts  9.74 us (9%)
  other arithmetic  3.27 us (3%)
  between operations  1.27 us (1%)
    ppermute x6, starting transfers between devices, swapped(): lax.ppermute(x, axis, [(i, i ^ 1 << bit) for i in range(lax.axis_size(axi...  22.8 us
    all_to_all x1, waiting for transfers between devices, shards(): lax.all_to_all(outgoing.reshape(param_count, slot_count, trace_count), 'p...  20.5 us
    ppermute x6, waiting for transfers between devices, swapped(): lax.ppermute(x, axis, [(i, i ^ 1 << bit) for i in range(lax.axis_size(axi...  19.8 us
    all_to_all x1, starting transfers between devices, shards(): lax.all_to_all(outgoing.reshape(param_count, slot_count, trace_count), 'p...  13 us
    sin x1, local copies, waits for them, and re-layouts, shards(): jnp.sin(angles)  8.47 us
    dot_general x12, matrix products, half(): jnp.einsum('rqk,kj->rqj', partner, lax.dynamic_index_in_dim(partner_map,...  4.77 us
    dot_general x6, matrix products, shards(): own = jnp.einsum('rqk,skj->srqj', kept_parts[i], own_map, precision=HIGH)  3.95 us
  transfers between devices with their start and end apart: 7, of which 5 were waited for; matrix products, arithmetic and copies ran while one was open for 16% of the time, Pallas kernels for 0%

profile of v5, /device:TPU:256, one launch (start us, length us, event | category | flops | bytes accessed | tf_op | source)
XLA Modules:
  0.0 105.9 jit_solution(16566068045070873879)
XLA Ops:
  0.0 0.0 copy-start
  0.8 1.0 fusion.6
  1.8 0.7 convert_add_fusion
  2.5 1.2 %reduce-precision_convert_fusion.1 = (bf16[512,256]{1,0:T(8,128)(2,1)S(1)}, bf16[512,256]{1,0:T(8,128)(2,1)S(1)}, bf16[512,256]{1,0:T(8,128)(2,1)S(1)}) fusion(f32[1,1,512,256]{3,2,1,0:T(8,128)} %param.7), kind=kLoop, calls=%fused_computation.43 | loop fusion | flops 917504 | bytes 1310720 | tf_op jit(solution)/shard_map/convert
  3.6 0.3 select_convert_fusion
  4.0 1.9 %fusion = f32[1024,256]{1,0:T(8,128)} fusion(bf16[1024,512]{1,0:T(8,128)(2,1)S(1)} %select_convert_fusion, bf16[512,256]{1,0:T(8,128)(2,1)S(1)} %get-tuple-element.54, bf16[512,256]{1,0:T(8,128)(2,1)S(1)} %get-tuple-element.55, bf16[512,256]{1,0:T(8,128)(2,1)S(1)} %get-tuple-element.53), kind=kOutput, calls=%fused_computation | convolution fusion | flops 817102848 | bytes 2883584 | tf_op jit(solution)/shard_map/dot_general | solution.py:58
  5.9 13.0 %all-to-all-start = ((f32[32,32,256]{2,1,0:T(8,128)}), f32[32,32,256]{2,1,0:T(8,128)S(1)}, u32[]{:S(2)}, u32[]{:S(2)}) async-start(f32[32,32,256]{2,1,0:T(8,128)} %bitcast.10), calls=%async_computation | async-start | bytes 2097152 | tf_op jit(solution)/shard_map/all_to_all | solution.py:59
  19.0 0.0 copy-done.4
  19.0 0.1 eq.52
  19.1 0.4 broadcast_compare_fusion
  19.4 8.5 %sine_bitcast_fusion = (f32[3,512,256]{2,1,0:T(8,128)}, f32[3,512,256]{2,1,0:T(8,128)}) fusion(f32[1,1,3,512,256]{4,3,2,1,0:T(8,128)} %param.13), kind=kLoop, calls=%fused_computation.8 | loop fusion | bytes 4718592 | tf_op jit(solution)/shard_map/sin | solution.py:67
  27.9 20.5 %all-to-all-done = f32[32,32,256]{2,1,0:T(8,128)S(1)} async-done(((f32[32,32,256]{2,1,0:T(8,128)}), f32[32,32,256]{2,1,0:T(8,128)S(1)}, u32[]{:S(2)}, u32[]{:S(2)}) %all-to-all-start) | async-done | bytes 1048608 | tf_op jit(solution)/shard_map/all_to_all | solution.py:59
  48.4 0.5 convolution_bitcast_fusion.5
  48.9 0.5 convolution_bitcast_fusion.7
  49.5 0.0 copy-start.1
  49.5 0.5 convolution_bitcast_fusion.6
  50.0 0.6 convolution_bitcast_fusion.4
  50.6 0.0 copy-done.1
  50.6 0.0 copy-start.3
  50.6 0.4 convolution_bitcast_fusion.2
  51.0 0.0 copy-start.2
  51.0 0.4 convolution_bitcast_fusion.3
  51.4 0.4 convolution_bitcast_fusion
  51.9 0.4 convolution_bitcast_fusion.1
  52.3 7.6 %collective-permute-start.3 = (f32[2,112,256]{2,1,0:T(8,128)S(1)}, f32[2,112,256]{2,1,0:T(8,128)S(1)}, u32[]{:S(2)}, u32[]{:S(2)}) collective-permute-start(f32[2,112,256]{2,1,0:T(8,128)S(1)} %convolution_bitcast_fusion.2), channel_id=1, source_target_pairs={{0,32},{32,0},{64,96},{96,64},{128,160},{160,128},{192,224},{224,1... | collective-permute-start | bytes 688136 | tf_op jit(solution)/shard_map/ppermute | solution.py:16
  60.0 1.9 %collective-permute-start = (f32[2,144,256]{2,1,0:T(8,128)S(1)}, f32[2,144,256]{2,1,0:T(8,128)S(1)}, u32[]{:S(2)}, u32[]{:S(2)}) collective-permute-start(f32[2,144,256]{2,1,0:T(8,128)S(1)} %convolution_bitcast_fusion), channel_id=1, source_target_pairs={{0,32},{32,0},{64,96},{96,64},{128,160},{160,128},{192,224},{224,1... | collective-permute-start | bytes 884744 | tf_op jit(solution)/shard_map/ppermute | solution.py:16
  61.9 0.0 copy-done.3
  61.9 0.1 fusion.92
  62.1 0.7 fusion.19
  62.8 0.6 fusion.17
  63.4 2.5 %collective-permute-done.3 = f32[2,112,256]{2,1,0:T(8,128)S(1)} collective-permute-done((f32[2,112,256]{2,1,0:T(8,128)S(1)}, f32[2,112,256]{2,1,0:T(8,128)S(1)}, u32[]{:S(2)}, u32[]{:S(2)}) %collective-permute-start.3) | collective-permute-done | bytes 229408 | tf_op jit(solution)/shard_map/ppermute | solution.py:16
  65.9 0.4 convolution_add_fusion.10
  66.3 0.4 convolution_add_fusion.11
  66.7 0.1 multiply_subtract_fusion.11
  66.8 1.9 %collective-permute-start.4 = (f32[2,112,256]{2,1,0:T(8,128)S(1)}, f32[2,112,256]{2,1,0:T(8,128)S(1)}, u32[]{:S(2)}, u32[]{:S(2)}) collective-permute-start(f32[2,112,256]{2,1,0:T(8,128)S(1)} %pad_maximum_fusion.2), channel_id=1, source_target_pairs={{0,64},{32,96},{64,0},{96,32},{128,192},{160,224},{192,128},{224,1... | collective-permute-start | bytes 688136 | tf_op jit(solution)/shard_map/ppermute | solution.py:16
  68.7 0.6 fusion.21
  69.4 2.9 %collective-permute-done = f32[2,144,256]{2,1,0:T(8,128)S(1)} collective-permute-done((f32[2,144,256]{2,1,0:T(8,128)S(1)}, f32[2,144,256]{2,1,0:T(8,128)S(1)}, u32[]{:S(2)}, u32[]{:S(2)}) %collective-permute-start) | collective-permute-done | bytes 294944 | tf_op jit(solution)/shard_map/ppermute | solution.py:16
  72.2 0.4 convolution_add_fusion.4
  72.7 0.4 convolution_add_fusion.5
  73.1 0.1 multiply_subtract_fusion.5
  73.2 2.1 %collective-permute-start.1 = (f32[2,144,256]{2,1,0:T(8,128)S(1)}, f32[2,144,256]{2,1,0:T(8,128)S(1)}, u32[]{:S(2)}, u32[]{:S(2)}) collective-permute-start(f32[2,144,256]{2,1,0:T(8,128)S(1)} %pad_maximum_fusion), channel_id=1, source_target_pairs={{0,64},{32,96},{64,0},{96,32},{128,192},{160,224},{192,128},{224,1... | collective-permute-start | bytes 884744 | tf_op jit(solution)/shard_map/ppermute | solution.py:16
  75.4 0.7 fusion.23
  76.1 9.4 %collective-permute-done.4 = f32[2,112,256]{2,1,0:T(8,128)S(1)} collective-permute-done((f32[2,112,256]{2,1,0:T(8,128)S(1)}, f32[2,112,256]{2,1,0:T(8,128)S(1)}, u32[]{:S(2)}, u32[]{:S(2)}) %collective-permute-start.4) | collective-permute-done | bytes 229408 | tf_op jit(solution)/shard_map/ppermute | solution.py:16
  85.5 0.4 convolution_add_fusion.8
  85.9 0.4 convolution_add_fusion.9
  86.3 0.1 multiply_subtract_fusion.9
  86.4 5.2 %collective-permute-start.5 = (f32[2,112,256]{2,1,0:T(8,128)S(1)}, f32[2,112,256]{2,1,0:T(8,128)S(1)}, u32[]{:S(2)}, u32[]{:S(2)}) collective-permute-start(f32[2,112,256]{2,1,0:T(8,128)S(1)} %pad_maximum_fusion.3), channel_id=1, source_target_pairs={{0,128},{32,160},{64,192},{96,224},{128,0},{160,32},{192,64},{224,... | collective-permute-start | bytes 688136 | tf_op jit(solution)/shard_map/ppermute | solution.py:16
  91.6 0.6 fusion.25
  92.2 0.0 collective-permute-done.1
  92.2 0.4 convolution_add_fusion.2
  92.6 0.4 convolution_add_fusion.3
  93.1 0.1 multiply_subtract_fusion.3
  93.2 4.0 %collective-permute-start.2 = (f32[2,144,256]{2,1,0:T(8,128)S(1)}, f32[2,144,256]{2,1,0:T(8,128)S(1)}, u32[]{:S(2)}, u32[]{:S(2)}) collective-permute-start(f32[2,144,256]{2,1,0:T(8,128)S(1)} %pad_maximum_fusion.1), channel_id=1, source_target_pairs={{0,128},{32,160},{64,192},{96,224},{128,0},{160,32},{192,64},{224,... | collective-permute-start | bytes 884744 | tf_op jit(solution)/shard_map/ppermute | solution.py:16
  97.2 0.7 fusion.27
  98.0 0.0 collective-permute-done.5
  98.0 0.4 convolution_add_fusion.7
  98.3 0.4 convolution_add_fusion.6
  98.7 0.1 multiply_subtract_fusion.7
  98.8 4.9 %collective-permute-done.2 = f32[2,144,256]{2,1,0:T(8,128)S(1)} collective-permute-done((f32[2,144,256]{2,1,0:T(8,128)S(1)}, f32[2,144,256]{2,1,0:T(8,128)S(1)}, u32[]{:S(2)}, u32[]{:S(2)}) %collective-permute-start.2) | collective-permute-done | bytes 294944 | tf_op jit(solution)/shard_map/ppermute | solution.py:16
  103.7 0.4 convolution_add_fusion
  104.2 0.4 convolution_add_fusion.1
  104.6 0.1 multiply_subtract_fusion.1
  104.7 0.1 maximum_maximum_fusion
  104.8 1.0 copy.17
  (13 shorter events, 0.2 us)
Async XLA Ops:
  0.0 62.0 %copy-start = (f32[2,512,256]{2,1,0:T(8,128)S(1)}, f32[2,512,256]{2,1,0:T(8,128)}, u32[]{:S(2)}) copy-start(f32[2,512,256]{2,1,0:T(8,128)} %param.12) | copy-start | bytes 3145732
  5.9 13.0 %copy-start.4 = (s32[1,1,32,32]{3,2,1,0:T(8,128)S(1)}, s32[1,1,32,32]{3,2,1,0:T(8,128)}, u32[]{:S(2)}) copy-start(s32[1,1,32,32]{3,2,1,0:T(8,128)} %param.10) | copy-start | bytes 12292
  5.9 42.4 %all-to-all-start = ((f32[32,32,256]{2,1,0:T(8,128)}), f32[32,32,256]{2,1,0:T(8,128)S(1)}, u32[]{:S(2)}, u32[]{:S(2)}) async-start(f32[32,32,256]{2,1,0:T(8,128)} %bitcast.10), calls=%async_computation | async-start | bytes 2097152 | tf_op jit(solution)/shard_map/all_to_all | solution.py:59
  49.5 1.1 %copy-start.1 = (f32[256,512]{1,0:T(8,128)S(1)}, f32[256,512]{1,0:T(8,128)}, u32[]{:S(2)}) copy-start(f32[256,512]{1,0:T(8,128)} %param.11) | copy-start | bytes 1572868
  50.6 11.3 %copy-start.3 = (f32[3,512,256]{2,1,0:T(8,128)S(1)}, f32[3,512,256]{2,1,0:T(8,128)}, u32[]{:S(2)}) copy-start(f32[3,512,256]{2,1,0:T(8,128)} %get-tuple-element.9) | copy-start | bytes 4718596
  51.0 10.9 %copy-start.2 = (f32[3,512,256]{2,1,0:T(8,128)S(1)}, f32[3,512,256]{2,1,0:T(8,128)}, u32[]{:S(2)}) copy-start(f32[3,512,256]{2,1,0:T(8,128)} %get-tuple-element.10) | copy-start | bytes 4718596
  52.3 13.6 %collective-permute-start.3 = (f32[2,112,256]{2,1,0:T(8,128)S(1)}, f32[2,112,256]{2,1,0:T(8,128)S(1)}, u32[]{:S(2)}, u32[]{:S(2)}) collective-permute-start(f32[2,112,256]{2,1,0:T(8,128)S(1)} %convolution_bitcast_fusion.2), channel_id=1, source_target_pairs={{0,32},{32,0},{64,96},{96,64},{128,160},{160,128},{192,224},{224,1... | collective-permute-start | bytes 688136 | tf_op jit(solution)/shard_map/ppermute | solution.py:16
  60.0 12.3 %collective-permute-start = (f32[2,144,256]{2,1,0:T(8,128)S(1)}, f32[2,144,256]{2,1,0:T(8,128)S(1)}, u32[]{:S(2)}, u32[]{:S(2)}) collective-permute-start(f32[2,144,256]{2,1,0:T(8,128)S(1)} %convolution_bitcast_fusion), channel_id=1, source_target_pairs={{0,32},{32,0},{64,96},{96,64},{128,160},{160,128},{192,224},{224,1... | collective-permute-start | bytes 884744 | tf_op jit(solution)/shard_map/ppermute | solution.py:16
  66.8 18.7 %collective-permute-start.4 = (f32[2,112,256]{2,1,0:T(8,128)S(1)}, f32[2,112,256]{2,1,0:T(8,128)S(1)}, u32[]{:S(2)}, u32[]{:S(2)}) collective-permute-start(f32[2,112,256]{2,1,0:T(8,128)S(1)} %pad_maximum_fusion.2), channel_id=1, source_target_pairs={{0,64},{32,96},{64,0},{96,32},{128,192},{160,224},{192,128},{224,1... | collective-permute-start | bytes 688136 | tf_op jit(solution)/shard_map/ppermute | solution.py:16
  73.2 19.0 %collective-permute-start.1 = (f32[2,144,256]{2,1,0:T(8,128)S(1)}, f32[2,144,256]{2,1,0:T(8,128)S(1)}, u32[]{:S(2)}, u32[]{:S(2)}) collective-permute-start(f32[2,144,256]{2,1,0:T(8,128)S(1)} %pad_maximum_fusion), channel_id=1, source_target_pairs={{0,64},{32,96},{64,0},{96,32},{128,192},{160,224},{192,128},{224,1... | collective-permute-start | bytes 884744 | tf_op jit(solution)/shard_map/ppermute | solution.py:16
  86.4 11.6 %collective-permute-start.5 = (f32[2,112,256]{2,1,0:T(8,128)S(1)}, f32[2,112,256]{2,1,0:T(8,128)S(1)}, u32[]{:S(2)}, u32[]{:S(2)}) collective-permute-start(f32[2,112,256]{2,1,0:T(8,128)S(1)} %pad_maximum_fusion.3), channel_id=1, source_target_pairs={{0,128},{32,160},{64,192},{96,224},{128,0},{160,32},{192,64},{224,... | collective-permute-start | bytes 688136 | tf_op jit(solution)/shard_map/ppermute | solution.py:16
  93.2 10.5 %collective-permute-start.2 = (f32[2,144,256]{2,1,0:T(8,128)S(1)}, f32[2,144,256]{2,1,0:T(8,128)S(1)}, u32[]{:S(2)}, u32[]{:S(2)}) collective-permute-start(f32[2,144,256]{2,1,0:T(8,128)S(1)} %pad_maximum_fusion.1), channel_id=1, source_target_pairs={{0,128},{32,160},{64,192},{96,224},{128,0},{160,32},{192,64},{224,... | collective-permute-start | bytes 884744 | tf_op jit(solution)/shard_map/ppermute | solution.py:16
